TPU v7x, 512 devices: a whole 4x4x16 slice. The times are simulated.
512 devices in a mesh: dp: 64 (over z, x_hi, core), fsdp: 8 (over x_lo, y).
Axes of the slice: x: 4 (x_hi: 2, x_lo: 2; x = x_hi * 2 + x_lo), y: 4, z: 16, core: 2. Of those that a mesh axis runs over, the one named last changes fastest.
Arguments:
- states: bfloat16 [128, 512, 5120], P('dp', None, 'fsdp'), may hold values from -240 to 240
- valid_counts: int32 [128], P('dp'), may hold values from 32 to 512
- section_ids: int32 [128], replicated, may hold values from 0 to 63, never falling along the last dimension, each value on 1 to 6 neighbouring positions
- norm_gain: bfloat16 [5120], P('fsdp'), may hold values from 0.099609375 to 1.8984375
- head_weight: bfloat16 [5120, 2048], P('fsdp'), may hold values from -0.078125 to 0.078125
Outputs:
- embeddings: float32 [64, 3840], P('dp')
Inputs may be any that keep to these rules, and one draw needn't show every extreme that they name: `section_ids`: section numbers never fall along the spans; every one of the 64 sections has 1 to 6 spans.
All inputs are finite; a program needn't handle non-finite values.
Results may differ from a plain program's by a relative error of at most 0.0003.
Values sent between devices are 32-bit elements; how exact they have to be, the bound alone decides.
No kernel may reach another device: no remote copies, remote signals or barrier semaphores. Data moves between devices by JAX's collectives and lax.ppermute only.
A program may use at most 64 MiB of HBM per device.

v0:
```python
import jax
import jax.numpy as jnp
from jax import lax
from jax.sharding import PartitionSpec as P

D = 5120


epsilon = 1e-06


def nested(projected):
    width = projected.shape[1]
    pieces = []
    for level in (width // 8, width // 4, width // 2, width):
        front = projected[:, :level]
        pieces.append(front * lax.rsqrt(jnp.mean(front * front, axis=1, keepdims=True) + epsilon))
    return jnp.concatenate(pieces, axis=1)


def local(states, valid_counts, section_ids, norm_gain, head_weight):
    values = states.astype(jnp.float32)
    partial_squares = jnp.sum(values * values, axis=-1)
    squares = lax.psum(partial_squares, "fsdp")
    scale = lax.rsqrt(squares / D + epsilon)
    slots = jnp.arange(states.shape[1], dtype=jnp.int32)
    used = (slots[None, :] < valid_counts[:, None]).astype(jnp.float32)
    weights = scale * used
    sums = jnp.einsum("cl,cld->cd", weights, values, precision=lax.Precision.HIGHEST)
    pooled = (
        sums / valid_counts.astype(jnp.float32)[:, None] * norm_gain.astype(jnp.float32)[None, :]
    )
    groups = lax.axis_size("dp")
    local_spans = pooled.shape[0]
    sec_local = local_spans // 2
    total_sections = sec_local * groups
    labels = jnp.arange(total_sections, dtype=jnp.int32)
    columns = lax.all_to_all(pooled, "dp", split_axis=1, concat_axis=0, tiled=True)
    member = (section_ids[None, :] == labels[:, None]).astype(jnp.float32)
    section_sums = jnp.dot(member, columns, precision=lax.Precision.HIGHEST)
    width = columns.shape[1]
    weight_part = lax.dynamic_slice_in_dim(head_weight, lax.axis_index("dp") * width, width, 0)
    weight_rows = weight_part.astype(jnp.float32)
    terms = jnp.dot(section_sums, weight_rows, precision=lax.Precision.HIGHEST)
    summed = lax.psum(terms, ("dp", "fsdp"))
    start = lax.axis_index("dp") * sec_local
    projected = lax.dynamic_slice_in_dim(summed, start, sec_local, 0)
    return nested(projected)


def solution(mesh):
    in_specs = (P("dp", None, "fsdp"), P("dp"), P(), P("fsdp"), P("fsdp", None))
    out_specs = P("dp", None)
    return jax.shard_map(local, mesh=mesh, in_specs=in_specs, out_specs=out_specs, check_vma=False)
```

profile of v0, /device:TPU:2, one launch (start us, length us, event | category | flops | bytes accessed | tf_op | source)
XLA Modules:
  0.0 533.8 jit_solution(12853491107874853173)
XLA Ops:
  6.5 0.0 copy-start
  6.5 0.0 copy-start.1
  6.5 0.8 convert_element_type.13
  7.4 0.7 convert_element_type.14
  8.0 1.6 multiply_reduce_fusion
  9.7 18.9 %psum.14 = f32[2,512]{1,0:T(2,128)S(1)} all-reduce(f32[2,512]{1,0:T(2,128)S(1)} %multiply_reduce_fusion), channel_id=1, replica_groups=mesh['dp'=64,'fsdp'=8] {'fsdp'}, use_global_device_ids=true, to_apply=%region_1.0 | all-reduce | flops 1024 | bytes 8192 | tf_op jit(solution)/shard_map/psum | solution.py:24
  28.6 0.7 fusion.5
  29.3 1.9 fusion.6
  31.3 0.1 fusion.4
  31.4 0.1 all_to_all.14
  31.5 0.7 copy.7
  32.2 18.0 %all-to-all-start = ((f32[2,64,10]{2,0,1:T(2,128)}), f32[2,64,10]{2,0,1:T(2,128)S(1)}, u32[]{:S(2)}, u32[]{:S(2)}) async-start(f32[2,64,10]{2,0,1:T(2,128)} %copy.7), calls=%async_computation | async-start | bytes 131072 | tf_op jit(solution)/shard_map/all_to_all | solution.py:38
  50.1 0.0 all-reduce.2.cloned.1.call-start
  50.2 15.8 %all-to-all-done = f32[2,64,10]{2,0,1:T(2,128)S(1)} async-done(((f32[2,64,10]{2,0,1:T(2,128)}), f32[2,64,10]{2,0,1:T(2,128)S(1)}, u32[]{:S(2)}, u32[]{:S(2)}) %all-to-all-start) | async-done | bytes 5152 | tf_op jit(solution)/shard_map/all_to_all | solution.py:38
  66.0 0.0 copy-done.1
  66.0 0.2 fusion.2
  66.2 0.0 copy-done
  66.2 1.2 fusion
  67.5 0.0 all-reduce.2.cloned.1.call-update
  67.5 447.5 %all-reduce.2.cloned.1.call-done = f32[64,2048]{1,0:T(8,128)} async-done(((f32[64,2048]{1,0:T(8,128)}), f32[64,2048]{1,0:T(8,128)}) %all-reduce.2.cloned.1.call-update) | async-done | bytes 524304 | tf_op jit(solution)/shard_map/psum | solution.py:45
  515.0 1.5 multiply_reduce_fusion.1
  517.1 1.4 multiply_reduce_fusion.2
  519.2 1.3 multiply_reduce_fusion.3
  521.2 1.3 multiply_reduce_fusion.4
  523.2 0.7 broadcast_multiply_fusion.3
  524.0 0.7 broadcast_multiply_fusion.2
  524.7 0.8 broadcast_multiply_fusion.1
  525.4 0.9 broadcast_multiply_fusion
  526.3 0.6 pad_maximum_fusion
Async XLA Ops:
  6.5 59.7 %copy-start = (bf16[640,2048]{1,0:T(8,128)(2,1)S(1)}, bf16[640,2048]{1,0:T(8,128)(2,1)}, u32[]{:S(2)}) copy-start(bf16[640,2048]{1,0:T(8,128)(2,1)} %param.9) | copy-start | bytes 7864324
  6.5 59.5 %copy-start.1 = (s32[128]{0:T(128)S(1)}, s32[128]{0:T(128)}, u32[]{:S(2)}) copy-start(s32[128]{0:T(128)} %param.7) | copy-start | bytes 1540
  32.2 33.8 %all-to-all-start = ((f32[2,64,10]{2,0,1:T(2,128)}), f32[2,64,10]{2,0,1:T(2,128)S(1)}, u32[]{:S(2)}, u32[]{:S(2)}) async-start(f32[2,64,10]{2,0,1:T(2,128)} %copy.7), calls=%async_computation | async-start | bytes 131072 | tf_op jit(solution)/shard_map/all_to_all | solution.py:38
  50.1 464.8 %all-reduce.2.cloned.1.call-start = ((), (), s32[]{:S(2)}) async-start(), calls=%async_computation.1 | async-start | bytes 1048576 | tf_op jit(solution)/shard_map/psum | solution.py:45
Sparse Core Ops, SparseCore 0:
  67.6 447.3 all-reduce.1
where the time goes:
time: 535 us; the launch traced here: 534 us
  waiting for transfers between devices  463 us (87%)
  blocking collectives  18.9 us (4%)
  starting transfers between devices  18 us (3%)
  between operations  16.2 us (3%)
  other arithmetic  13.1 us (2%)
    psum x1, waiting for transfers between devices, local(): summed = lax.psum(terms, ('dp', 'fsdp'))  447 us
    psum x1, blocking collectives, local(): squares = lax.psum(partial_squares, 'fsdp')  18.9 us
    all_to_all x1, starting transfers between devices, local(): lax.all_to_all(pooled, 'dp', split_axis=1, concat_axis=0, tiled=True)  18 us
    all_to_all x1, waiting for transfers between devices, local(): lax.all_to_all(pooled, 'dp', split_axis=1, concat_axis=0, tiled=True)  15.8 us
  transfers between devices with their start and end apart: 2, of which 2 were waited for; matrix products, arithmetic and copies ran while one was open for 0% of the time, Pallas kernels for 0%

commit v1 on v0

--- a/solution.py
+++ b/solution.py
@@ -34,17 +34,16 @@
     local_spans = pooled.shape[0]
     sec_local = local_spans // 2
     total_sections = sec_local * groups
+    me = lax.axis_index("dp")
+    my_ids = lax.dynamic_slice_in_dim(section_ids, me * local_spans, local_spans, 0)
     labels = jnp.arange(total_sections, dtype=jnp.int32)
-    columns = lax.all_to_all(pooled, "dp", split_axis=1, concat_axis=0, tiled=True)
-    member = (section_ids[None, :] == labels[:, None]).astype(jnp.float32)
-    section_sums = jnp.dot(member, columns, precision=lax.Precision.HIGHEST)
-    width = columns.shape[1]
-    weight_part = lax.dynamic_slice_in_dim(head_weight, lax.axis_index("dp") * width, width, 0)
-    weight_rows = weight_part.astype(jnp.float32)
-    terms = jnp.dot(section_sums, weight_rows, precision=lax.Precision.HIGHEST)
-    summed = lax.psum(terms, ("dp", "fsdp"))
-    start = lax.axis_index("dp") * sec_local
-    projected = lax.dynamic_slice_in_dim(summed, start, sec_local, 0)
+    contrib = jnp.zeros((total_sections, pooled.shape[1]), jnp.float32)
+    for c in range(local_spans):
+        contrib = contrib + jnp.where((labels == my_ids[c])[:, None], pooled[c][None, :], 0.0)
+    received = lax.all_to_all(contrib, "dp", 0, 0, tiled=True)
+    section_sums = jnp.sum(received.reshape(groups, sec_local, -1), axis=0)
+    terms = jnp.dot(section_sums, head_weight.astype(jnp.float32), precision=lax.Precision.HIGHEST)
+    projected = lax.psum(terms, "fsdp")
     return nested(projected)
 
 

time: 535 us -> 90.5 us (0.17)
  the two profiles are of different devices: /device:TPU:2 before, /device:TPU:8 now
where the time goes in v1:
time: 90.5 us; the launch traced here: 90.2 us
  blocking collectives  74.2 us (82%)
  other arithmetic  8.81 us (10%)
  matrix products  3.06 us (3%)
  between operations  2.77 us (3%)
  local copies, waits for them, and re-layouts  1.36 us (2%)
    all_to_all x1, blocking collectives, local(): received = lax.all_to_all(contrib, 'dp', 0, 0, tiled=True)  32.8 us
    psum x1, blocking collectives, local(): squares = lax.psum(partial_squares, 'fsdp')  21.8 us
    psum x1, blocking collectives, local(): projected = lax.psum(terms, 'fsdp')  19.6 us
    reduce_sum x4, other arithmetic, nested(): jnp.mean(front * front, axis=1, keepdims=True) + epsilon  2.53 us
    dot_general x1, matrix products, local(): jnp.einsum('cl,cld->cd', weights, values, precision=lax.Precision.HIGHEST)  1.94 us

profile of v1, /device:TPU:8, one launch (start us, length us, event | category | flops | bytes accessed | tf_op | source)
XLA Modules:
  0.0 90.2 jit_solution(11067146023472021934)
XLA Ops:
  0.0 0.0 copy-start
  0.0 0.8 convert_element_type.12
  0.8 0.7 dynamic_slice.3
  1.5 0.6 fusion.5
  2.1 0.7 convert_element_type.13
  2.8 1.6 %multiply_reduce_fusion = f32[2,512]{1,0:T(2,128)S(1)} fusion(bf16[2,512,640]{2,1,0:T(8,128)(2,1)} %param.5), kind=kLoop, calls=%fused_computation | loop fusion | flops 1965056 | bytes 1314816 | tf_op jit(solution)/shard_map/reduce_sum | solution.py:23
  4.5 21.8 %psum.14 = f32[2,512]{1,0:T(2,128)S(1)} all-reduce(f32[2,512]{1,0:T(2,128)S(1)} %multiply_reduce_fusion), channel_id=1, replica_groups=mesh['dp'=64,'fsdp'=8] {'fsdp'}, use_global_device_ids=true, to_apply=%region_1.0 | all-reduce | flops 1024 | bytes 8192 | tf_op jit(solution)/shard_map/psum | solution.py:24
  26.2 0.7 fusion.2
  27.0 1.9 %fusion.3 = f32[2,1,640]{2,1,0:T(1,128)S(1)} fusion(bf16[2,512,640]{2,1,0:T(8,128)(2,1)} %param.5, f32[2,512,1]{1,0,2:T(2,128)S(1)} %fusion.2), kind=kOutput, calls=%fused_computation.10 | convolution fusion | flops 7864320 | bytes 1319936 | tf_op jit(solution)/shard_map/cl,cld->cd/dot_general | solution.py:29
  28.9 0.1 fusion.1
  29.0 1.3 %iota_compare_fusion = (pred[64]{0:T(512)(128)(4,1)S(1)}, pred[64]{0:T(512)(128)(4,1)S(1)}) fusion(s32[]{:T(128)} %bitcast.3, s32[]{:T(128)} %bitcast), kind=kLoop, calls=%fused_computation.21 | loop fusion | flops 128 | bytes 136 | tf_op jit(solution)/shard_map/eq | solution.py:42
  30.3 0.2 fusion
  30.6 32.8 %all_to_all.6 = f32[64,1,640]{2,1,0:T(1,128)S(1)} all-to-all(f32[64,1,640]{2,1,0:T(1,128)S(1)} %fusion), channel_id=1, replica_groups=mesh['dp'=64,'fsdp'=8] {'dp'}, dimensions={0} | all-to-all | bytes 327680 | tf_op jit(solution)/shard_map/all_to_all | solution.py:43
  63.4 0.1 reduce_sum.55
  63.6 0.0 copy-done
  63.6 1.1 %fusion.6 = f32[1,2048]{1,0:T(1,128)S(1)} fusion(f32[640,1]{0,1:T(1,128)S(1)} %reshape.153, bf16[640,2048]{1,0:T(8,128)(2,1)S(1)} %copy-done), kind=kOutput, calls=%fused_computation.24 | convolution fusion | flops 15728640 | bytes 2632192 | tf_op jit(solution)/shard_map/dot_general | solution.py:45
  64.7 19.6 %psum.15 = f32[1,2048]{1,0:T(1,128)S(1)} all-reduce(f32[1,2048]{1,0:T(1,128)S(1)} %fusion.6), channel_id=1, replica_groups=mesh['dp'=64,'fsdp'=8] {'fsdp'}, use_global_device_ids=true, to_apply=%region_3.4 | all-reduce | flops 2048 | bytes 16384 | tf_op jit(solution)/shard_map/psum | solution.py:46
  84.3 0.6 multiply_reduce_fusion.1
  84.9 0.7 multiply_reduce_fusion.2
  85.6 0.6 multiply_reduce_fusion.3
  86.2 0.6 multiply_reduce_fusion.4
  89.5 0.6 pad_maximum_fusion
  (6 shorter events, 0.1 us)
Async XLA Ops:
  0.0 63.6 %copy-start = (bf16[640,2048]{1,0:T(8,128)(2,1)S(1)}, bf16[640,2048]{1,0:T(8,128)(2,1)}, u32[]{:S(2)}) copy-start(bf16[640,2048]{1,0:T(8,128)(2,1)} %param.9) | copy-start | bytes 7864324

commit v2 on v1

v2 whole, which is shorter than its diff:
```python
import jax
import jax.numpy as jnp
from jax import lax
from jax.experimental import pallas as pl
from jax.sharding import Mesh, PartitionSpec as P

D = 5120


epsilon = 1e-06


def nested_kernel(x_ref, o_ref):
    x = x_ref[...]
    width = x.shape[1]
    squared = x * x
    offset = 0
    for level in (width // 8, width // 4, width // 2, width):
        mean = jnp.sum(squared[:, :level], axis=1, keepdims=True) / level
        o_ref[:, offset:offset + level] = x[:, :level] * lax.rsqrt(mean + epsilon)
        offset += level


def nested(projected):
    rows, width = projected.shape
    out = jax.ShapeDtypeStruct((rows, width // 8 + width // 4 + width // 2 + width), jnp.float32)
    return pl.pallas_call(nested_kernel, out_shape=out)(projected)


def fsdp_sum(x):
    return lax.psum(lax.psum(x, "y"), "xl")


def local(states, valid_counts, section_ids, norm_gain, head_weight):
    values = states.astype(jnp.float32)
    partial_squares = jnp.sum(values * values, axis=-1)
    squares = fsdp_sum(partial_squares)
    scale = lax.rsqrt(squares / D + epsilon)
    slots = jnp.arange(states.shape[1], dtype=jnp.int32)
    used = (slots[None, :] < valid_counts[:, None]).astype(jnp.float32)
    weights = scale * used
    sums = jnp.einsum("cl,cld->cd", weights, values, precision=lax.Precision.HIGHEST)
    pooled = (
        sums / valid_counts.astype(jnp.float32)[:, None] * norm_gain.astype(jnp.float32)[None, :]
    )
    groups = lax.axis_size("dp")
    local_spans = pooled.shape[0]
    sec_local = local_spans // 2
    total_sections = sec_local * groups
    me = lax.axis_index("dp")
    my_ids = lax.dynamic_slice_in_dim(section_ids, me * local_spans, local_spans, 0)
    labels = jnp.arange(total_sections, dtype=jnp.int32)
    contrib = jnp.zeros((total_sections, pooled.shape[1]), jnp.float32)
    for c in range(local_spans):
        contrib = contrib + jnp.where((labels == my_ids[c])[:, None], pooled[c][None, :], 0.0)
    received = lax.all_to_all(contrib, "dp", 0, 0, tiled=True)
    section_sums = jnp.sum(received.reshape(groups, sec_local, -1), axis=0)
    terms = jnp.dot(section_sums, head_weight.astype(jnp.float32), precision=lax.Precision.HIGHEST)
    projected = fsdp_sum(terms)
    return nested(projected)


def solution(mesh):
    dp, fsdp = mesh.shape["dp"], mesh.shape["fsdp"]
    fine = Mesh(mesh.devices.reshape(dp, 2, fsdp // 2), ("dp", "xl", "y"))
    features = ("xl", "y")
    in_specs = (P("dp", None, features), P("dp"), P(), P(features), P(features, None))
    out_specs = P("dp", None)
    return jax.shard_map(local, mesh=fine, in_specs=in_specs, out_specs=out_specs, check_vma=False)
```

time: 90.5 us -> 79.4 us (0.88)
  blocking collectives: 74.2 us -> 67.5 us
  other arithmetic: 8.81 us -> 5.64 us
  between operations: 2.77 us -> 0.05 us
  Pallas kernels: 0 us -> 1.4 us
    psum x2 -> x4, blocking collectives: 41.3 us -> 34.4 us  [fsdp_sum(): return lax.psum(lax.psum(x, 'y'), 'xl')]
    reduce_sum x4 -> x0, other arithmetic: 2.53 us -> none  [nested(): jnp.mean(front * front, axis=1, keepdims=True) + epsilon]
    pallas_call x0 -> x1, Pallas kernels: none -> 1.4 us  [nested(): return pl.pallas_call(nested_kernel, out_shape=out)(projected)]
where the time goes in v2:
time: 79.4 us; the launch traced here: 79 us
  blocking collectives  67.5 us (85%)
  other arithmetic  5.64 us (7%)
  matrix products  3.06 us (4%)
  Pallas kernels  1.4 us (2%)
  local copies, waits for them, and re-layouts  1.36 us (2%)
    psum x4, blocking collectives, fsdp_sum(): return lax.psum(lax.psum(x, 'y'), 'xl')  34.4 us
    all_to_all x1, blocking collectives, local(): received = lax.all_to_all(contrib, 'dp', 0, 0, tiled=True)  33.1 us
    dot_general x1, matrix products, local(): jnp.einsum('cl,cld->cd', weights, values, precision=lax.Precision.HIGHEST)  1.94 us
    reduce_sum x1, other arithmetic, local(): partial_squares = jnp.sum(values * values, axis=-1)  1.65 us

profile of v2, /device:TPU:8, one launch (start us, length us, event | category | flops | bytes accessed | tf_op | source)
XLA Modules:
  0.0 79.0 jit_solution(6996463642573500047)
XLA Ops:
  0.0 0.0 copy-start
  0.0 0.8 %convert_element_type.12 = f32[2]{0:T(128)S(1)} convert(s32[2]{0:T(128)} %param.6) | non-fusion elementwise | flops 2 | bytes 16 | tf_op jit(solution)/shard_map/convert_element_type | solution.py:44
  0.8 0.7 dynamic_slice.3
  1.5 0.6 fusion.5
  2.1 0.7 convert_element_type.13
  2.8 1.6 %multiply_reduce_fusion = f32[2,512]{1,0:T(2,128)S(1)} fusion(bf16[2,512,640]{2,1,0:T(8,128)(2,1)} %param.5), kind=kLoop, calls=%fused_computation | loop fusion | flops 1965056 | bytes 1314816 | tf_op jit(solution)/shard_map/reduce_sum | solution.py:36
  4.5 13.6 %psum.28 = f32[2,512]{1,0:T(2,128)S(1)} all-reduce(f32[2,512]{1,0:T(2,128)S(1)} %multiply_reduce_fusion), channel_id=1, replica_groups=mesh['dp'=64,'xl'=2,'y'=4] {'y'}, use_global_device_ids=true, to_apply=%region_1.0 | all-reduce | flops 1024 | bytes 8192 | tf_op jit(solution)/shard_map/psum | solution.py:31
  18.0 4.9 %psum.29 = f32[2,512]{1,0:T(2,128)S(1)} all-reduce(f32[2,512]{1,0:T(2,128)S(1)} %psum.28), channel_id=1, replica_groups=mesh['dp'=64,'xl'=2,'y'=4] {'xl'}, use_global_device_ids=true, to_apply=%region_2.0 | all-reduce | flops 1024 | bytes 8192 | tf_op jit(solution)/shard_map/psum | solution.py:31
  23.0 0.7 fusion.2
  23.7 1.9 %fusion.3 = f32[2,1,640]{2,1,0:T(1,128)S(1)} fusion(bf16[2,512,640]{2,1,0:T(8,128)(2,1)} %param.5, f32[2,512,1]{1,0,2:T(2,128)S(1)} %fusion.2), kind=kOutput, calls=%fused_computation.8 | convolution fusion | flops 7864320 | bytes 1319936 | tf_op jit(solution)/shard_map/cl,cld->cd/dot_general | solution.py:42
  25.6 0.1 fusion.1
  25.7 1.3 %iota_compare_fusion = (pred[64]{0:T(512)(128)(4,1)S(1)}, pred[64]{0:T(512)(128)(4,1)S(1)}) fusion(s32[]{:T(128)} %bitcast.3, s32[]{:T(128)} %bitcast), kind=kLoop, calls=%fused_computation.12 | loop fusion | flops 128 | bytes 136 | tf_op jit(solution)/shard_map/eq | solution.py:55
  27.1 0.2 fusion
  27.3 33.1 %all_to_all.6 = f32[64,1,640]{2,1,0:T(1,128)S(1)} all-to-all(f32[64,1,640]{2,1,0:T(1,128)S(1)} %fusion), channel_id=1, replica_groups=mesh['dp'=64,'xl'=2,'y'=4] {'dp'}, dimensions={0} | all-to-all | bytes 327680 | tf_op jit(solution)/shard_map/all_to_all | solution.py:56
  60.4 0.1 reduce_sum.19
  60.5 0.0 copy-done
  60.6 1.1 %fusion.6 = f32[1,2048]{1,0:T(1,128)S(1)} fusion(f32[640,1]{0,1:T(1,128)S(1)} %reshape.113, bf16[640,2048]{1,0:T(8,128)(2,1)S(1)} %copy-done), kind=kOutput, calls=%fused_computation.15 | convolution fusion | flops 15728640 | bytes 2632192 | tf_op jit(solution)/shard_map/dot_general | solution.py:58
  61.7 10.3 %psum.30 = f32[1,2048]{1,0:T(1,128)S(1)} all-reduce(f32[1,2048]{1,0:T(1,128)S(1)} %fusion.6), channel_id=1, replica_groups=mesh['dp'=64,'xl'=2,'y'=4] {'y'}, use_global_device_ids=true, to_apply=%region_4.5 | all-reduce | flops 2048 | bytes 16384 | tf_op jit(solution)/shard_map/psum | solution.py:31
  72.0 5.6 %psum.31.x_ref = f32[1,2048]{1,0:T(1,128)} all-reduce(f32[1,2048]{1,0:T(1,128)S(1)} %psum.30), channel_id=1, replica_groups=mesh['dp'=64,'xl'=2,'y'=4] {'xl'}, use_global_device_ids=true, to_apply=%region_5.6 | all-reduce | flops 2048 | bytes 16384 | tf_op jit(solution)/shard_map/psum | solution.py:31
  77.6 1.4 %shard_map.55 = f32[1,3840]{1,0:T(1,128)} custom-call(f32[1,2048]{1,0:T(1,128)} %psum.31.x_ref), custom_call_target="tpu_custom_call" | custom-call | tf_op jit(solution)/shard_map/pallas_call | solution.py:27
  (2 shorter events, 0.0 us)
Async XLA Ops:
  0.0 60.5 %copy-start = (bf16[640,2048]{1,0:T(8,128)(2,1)S(1)}, bf16[640,2048]{1,0:T(8,128)(2,1)}, u32[]{:S(2)}) copy-start(bf16[640,2048]{1,0:T(8,128)(2,1)} %param.9) | copy-start | bytes 7864324

commit v3 on v2

v3 whole, which is shorter than its diff:
```python
import jax
import jax.numpy as jnp
from jax import lax
from jax.experimental import pallas as pl
from jax.experimental.pallas import tpu as pltpu
from jax.sharding import Mesh, PartitionSpec as P

D = 5120


epsilon = 1e-06


def nested_kernel(x_ref, o_ref):
    x = x_ref[...]
    width = x.shape[1]
    squared = x * x
    offset = 0
    for level in (width // 8, width // 4, width // 2, width):
        mean = jnp.sum(squared[:, :level], axis=1, keepdims=True) / level
        o_ref[:, offset:offset + level] = x[:, :level] * lax.rsqrt(mean + epsilon)
        offset += level


def nested(projected):
    rows, width = projected.shape
    out = jax.ShapeDtypeStruct((rows, width // 8 + width // 4 + width // 2 + width), jnp.float32)
    return pl.pallas_call(nested_kernel, out_shape=out)(projected)


def fsdp_sum(x):
    return lax.psum(lax.psum(x, "y"), "xl")


def pool_kernel(counts_ref, ids_ref, states_ref, squares_ref, gain_ref, out_ref):
    spans, slots_n, _ = states_ref.shape
    me = lax.axis_index("dp")
    out_ref[...] = jnp.zeros(out_ref.shape, jnp.float32)
    gain = gain_ref[...].astype(jnp.float32)
    for c in range(spans):
        count = counts_ref[c]
        scale = lax.rsqrt(squares_ref[pl.ds(c, 1), :] / D + epsilon)
        slots = lax.broadcasted_iota(jnp.int32, scale.shape, 1)
        weights = jnp.where(slots < count, scale, 0.0)
        column = jnp.transpose(jnp.broadcast_to(weights, (128, slots_n)))[:, :1]
        values = states_ref[c].astype(jnp.float32)
        sums = jnp.sum(values * column, axis=0, keepdims=True)
        pooled = sums / count.astype(jnp.float32) * gain
        section = ids_ref[me * spans + c]
        out_ref[pl.ds(section, 1)] += pooled[None]


def local(states, valid_counts, section_ids, norm_gain, head_weight):
    values = states.astype(jnp.float32)
    partial_squares = jnp.sum(values * values, axis=-1)
    squares = fsdp_sum(partial_squares)
    groups = lax.axis_size("dp")
    local_spans, _, features = states.shape
    sec_local = local_spans // 2
    total_sections = sec_local * groups
    smem = pl.BlockSpec(memory_space=pltpu.SMEM)
    vmem = pl.BlockSpec(memory_space=pltpu.VMEM)
    contrib = pl.pallas_call(
        pool_kernel,
        out_shape=jax.ShapeDtypeStruct((total_sections, 1, features), jnp.float32),
        in_specs=[smem, smem, vmem, vmem, vmem],
        out_specs=vmem,
    )(valid_counts, section_ids, states, squares, norm_gain.reshape(1, features))
    received = lax.all_to_all(contrib, "dp", 0, 0, tiled=True)
    section_sums = jnp.sum(received.reshape(groups, sec_local, features), axis=0)
    terms = jnp.dot(section_sums, head_weight.astype(jnp.float32), precision=lax.Precision.HIGHEST)
    projected = fsdp_sum(terms)
    return nested(projected)


def solution(mesh):
    dp, fsdp = mesh.shape["dp"], mesh.shape["fsdp"]
    fine = Mesh(mesh.devices.reshape(dp, 2, fsdp // 2), ("dp", "xl", "y"))
    features = ("xl", "y")
    in_specs = (P("dp", None, features), P("dp"), P(), P(features), P(features, None))
    out_specs = P("dp", None)
    return jax.shard_map(local, mesh=fine, in_specs=in_specs, out_specs=out_specs, check_vma=False)
```

time: 79.4 us -> 76.8 us (0.967)
  other arithmetic: 5.64 us -> 1.77 us
  Pallas kernels: 1.4 us -> 3.91 us
  matrix products: 3.06 us -> 1.12 us
  blocking collectives: 67.5 us -> 68.3 us
    pallas_call x0 -> x1, Pallas kernels: none -> 2.51 us  [local(): pl.pallas_call(pool_kernel, out_shape=jax.ShapeDtypeStruct((total_section...]
    dot_general x1 -> x0, matrix products: 1.94 us -> none  [local(): jnp.einsum('cl,cld->cd', weights, values, precision=lax.Precision.HIGHEST)]
    convert_element_type x2 -> x0, other arithmetic: 1.49 us -> none  [the longest x1 0.81 us: local(): valid_counts.astype(jnp.float32)[:, None]]
    reshape x0 -> x1, local copies, waits for them, and re-layouts: none -> 1.39 us  [local(): norm_gain.reshape(1, features)]
    eq x1 -> x0, other arithmetic: 1.34 us -> none  [local(): labels == my_ids[c]]
    mul x2 -> x0, other arithmetic: 0.8 us -> none  [the longest x1 0.72 us: local(): weights = scale * used]
where the time goes in v3:
time: 76.8 us; the launch traced here: 76.5 us
  blocking collectives  68.3 us (89%)
  Pallas kernels  3.91 us (5%)
  other arithmetic  1.77 us (2%)
  local copies, waits for them, and re-layouts  1.4 us (2%)
  matrix products  1.12 us (1%)
    psum x4, blocking collectives, fsdp_sum(): return lax.psum(lax.psum(x, 'y'), 'xl')  35 us
    all_to_all x1, blocking collectives, local(): received = lax.all_to_all(contrib, 'dp', 0, 0, tiled=True)  33.3 us
    pallas_call x1, Pallas kernels, local(): pl.pallas_call(pool_kernel, out_shape=jax.ShapeDtypeStruct((total_section...  2.51 us
    reduce_sum x1, other arithmetic, local(): partial_squares = jnp.sum(values * values, axis=-1)  1.65 us

profile of v3, /device:TPU:8, one launch (start us, length us, event | category | flops | bytes accessed | tf_op | source)
XLA Modules:
  0.0 76.5 jit_solution(10914333826642639380)
XLA Ops:
  0.0 0.0 copy-start
  0.0 1.4 %reshape.7.gain_ref = bf16[1,640]{1,0:T(2,128)(2,1)} reshape(bf16[640]{0:T(1024)(128)(2,1)} %param.8) | data formatting | bytes 2560 | tf_op jit(solution)/shard_map/reshape | solution.py:68
  1.4 1.6 %multiply_reduce_fusion = f32[2,512]{1,0:T(2,128)S(1)} fusion(bf16[2,512,640]{2,1,0:T(8,128)(2,1)} %states_ref.1), kind=kLoop, calls=%fused_computation | loop fusion | flops 1965056 | bytes 1314816 | tf_op jit(solution)/shard_map/reduce_sum | solution.py:55
  3.0 13.6 %psum.28 = f32[2,512]{1,0:T(2,128)S(1)} all-reduce(f32[2,512]{1,0:T(2,128)S(1)} %multiply_reduce_fusion), channel_id=1, replica_groups=mesh['dp'=64,'xl'=2,'y'=4] {'y'}, use_global_device_ids=true, to_apply=%region_1.0 | all-reduce | flops 1024 | bytes 8192 | tf_op jit(solution)/shard_map/psum | solution.py:32
  16.6 5.5 %psum.29.squares_ref = f32[2,512]{1,0:T(2,128)} all-reduce(f32[2,512]{1,0:T(2,128)S(1)} %psum.28), channel_id=1, replica_groups=mesh['dp'=64,'xl'=2,'y'=4] {'xl'}, use_global_device_ids=true, to_apply=%region_2.0 | all-reduce | flops 1024 | bytes 8192 | tf_op jit(solution)/shard_map/psum | solution.py:32
  22.1 2.5 %shard_map.55 = f32[64,1,640]{2,1,0:T(1,128)} custom-call(s32[2]{0:T(128)} %counts_ref.1, s32[128]{0:T(128)} %ids_ref.1, bf16[2,512,640]{2,1,0:T(8,128)(2,1)} %states_ref.1, f32[2,512]{1,0:T(2,128)} %psum.29.squares_ref, bf16[1,640]{1,0:T(2,128)(2,1)} %reshape.7.gain_ref), custom_call_target="tpu_custom_call" | custom-call | tf_op jit(solution)/shard_map/pallas_call | solution.py:63
  24.6 33.3 %all_to_all.5 = f32[64,1,640]{2,1,0:T(1,128)S(1)} all-to-all(f32[64,1,640]{2,1,0:T(1,128)} %shard_map.55), channel_id=1, replica_groups=mesh['dp'=64,'xl'=2,'y'=4] {'dp'}, dimensions={0} | all-to-all | bytes 327680 | tf_op jit(solution)/shard_map/all_to_all | solution.py:69
  57.9 0.1 reduce_sum.19
  58.0 0.0 copy-done
  58.1 1.1 %fusion = f32[1,2048]{1,0:T(1,128)S(1)} fusion(f32[640,1]{0,1:T(1,128)S(1)} %reshape.8, bf16[640,2048]{1,0:T(8,128)(2,1)S(1)} %copy-done), kind=kOutput, calls=%fused_computation.1 | convolution fusion | flops 15728640 | bytes 2632192 | tf_op jit(solution)/shard_map/dot_general | solution.py:71
  59.2 10.3 %psum.30 = f32[1,2048]{1,0:T(1,128)S(1)} all-reduce(f32[1,2048]{1,0:T(1,128)S(1)} %fusion), channel_id=1, replica_groups=mesh['dp'=64,'xl'=2,'y'=4] {'y'}, use_global_device_ids=true, to_apply=%region_4.0 | all-reduce | flops 2048 | bytes 16384 | tf_op jit(solution)/shard_map/psum | solution.py:32
  69.5 5.6 %psum.31.x_ref = f32[1,2048]{1,0:T(1,128)} all-reduce(f32[1,2048]{1,0:T(1,128)S(1)} %psum.30), channel_id=1, replica_groups=mesh['dp'=64,'xl'=2,'y'=4] {'xl'}, use_global_device_ids=true, to_apply=%region_5.0 | all-reduce | flops 2048 | bytes 16384 | tf_op jit(solution)/shard_map/psum | solution.py:32
  75.1 1.4 %shard_map.56 = f32[1,3840]{1,0:T(1,128)} custom-call(f32[1,2048]{1,0:T(1,128)} %psum.31.x_ref), custom_call_target="tpu_custom_call" | custom-call | tf_op jit(solution)/shard_map/pallas_call | solution.py:28
  (1 shorter events, 0.0 us)
Async XLA Ops:
  0.0 58.0 %copy-start = (bf16[640,2048]{1,0:T(8,128)(2,1)S(1)}, bf16[640,2048]{1,0:T(8,128)(2,1)}, u32[]{:S(2)}) copy-start(bf16[640,2048]{1,0:T(8,128)(2,1)} %param.9) | copy-start | bytes 7864324

commit v4 on v3

v4 whole, which is shorter than its diff:
```python
import functools

import jax
import jax.numpy as jnp
from jax import lax
from jax.experimental import pallas as pl
from jax.experimental.pallas import tpu as pltpu
from jax.sharding import Mesh, PartitionSpec as P

D = 5120


epsilon = 1e-06


def nested_kernel(x_ref, o_ref):
    x = x_ref[...]
    width = x.shape[1]
    squared = x * x
    offset = 0
    for level in (width // 8, width // 4, width // 2, width):
        mean = jnp.sum(squared[:, :level], axis=1, keepdims=True) / level
        o_ref[:, offset:offset + level] = x[:, :level] * lax.rsqrt(mean + epsilon)
        offset += level


def nested(projected):
    rows, width = projected.shape
    out = jax.ShapeDtypeStruct((rows, width // 8 + width // 4 + width // 2 + width), jnp.float32)
    return pl.pallas_call(nested_kernel, out_shape=out)(projected)


def fsdp_sum(x):
    return lax.psum(lax.psum(x, "y"), "xl")


def pool_kernel(dp_shape, counts_ref, ids_ref, states_ref, squares_ref, out_ref):
    spans, slots_n, _ = states_ref.shape
    z_n, xh_n, c_n = dp_shape
    sec_local = out_ref.shape[0] // (z_n * xh_n * c_n)
    me = (lax.axis_index("z") * xh_n + lax.axis_index("xh")) * c_n + lax.axis_index("c")
    out_ref[...] = jnp.zeros(out_ref.shape, jnp.float32)
    for c in range(spans):
        count = counts_ref[c]
        scale = lax.rsqrt(squares_ref[pl.ds(c, 1), :] / D + epsilon)
        slots = lax.broadcasted_iota(jnp.int32, scale.shape, 1)
        weights = jnp.where(slots < count, scale, 0.0)
        column = jnp.transpose(jnp.broadcast_to(weights, (128, slots_n)))[:, :1]
        values = states_ref[c].astype(jnp.float32)
        sums = jnp.sum(values * column, axis=0, keepdims=True)
        pooled = sums / count.astype(jnp.float32)
        section = ids_ref[me * spans + c]
        owner = section // sec_local
        place = ((owner % c_n) * xh_n + (owner // c_n) % xh_n) * z_n + owner // (c_n * xh_n)
        row = place * sec_local + section % sec_local
        out_ref[pl.ds(row, 1)] += pooled[None]


def make_local(dp_shape):
    groups = dp_shape[0] * dp_shape[1] * dp_shape[2]

    def local(states, valid_counts, section_ids, norm_gain, head_weight):
        values = states.astype(jnp.float32)
        partial_squares = jnp.sum(values * values, axis=-1)
        squares = fsdp_sum(partial_squares)
        local_spans, _, features = states.shape
        sec_local = local_spans // 2
        total_sections = sec_local * groups
        smem = pl.BlockSpec(memory_space=pltpu.SMEM)
        vmem = pl.BlockSpec(memory_space=pltpu.VMEM)
        contrib = pl.pallas_call(
            functools.partial(pool_kernel, dp_shape),
            out_shape=jax.ShapeDtypeStruct((total_sections, 1, features), jnp.float32),
            in_specs=[smem, smem, vmem, vmem],
            out_specs=vmem,
        )(valid_counts, section_ids, states, squares)
        received = lax.all_to_all(contrib, ("c", "xh", "z"), 0, 0, tiled=True)
        section_sums = jnp.sum(received.reshape(groups, sec_local, features), axis=0)
        section_sums = section_sums * norm_gain.astype(jnp.float32)[None, :]
        terms = jnp.dot(section_sums, head_weight.astype(jnp.float32), precision=lax.Precision.HIGHEST)
        projected = fsdp_sum(terms)
        return nested(projected)

    return local


def solution(mesh):
    dp, fsdp = mesh.shape["dp"], mesh.shape["fsdp"]
    dp_shape = (dp // 4, 2, 2)
    fine = Mesh(mesh.devices.reshape(*dp_shape, 2, fsdp // 2), ("z", "xh", "c", "xl", "y"))
    spans = ("z", "xh", "c")
    features = ("xl", "y")
    in_specs = (P(spans, None, features), P(spans), P(), P(features), P(features, None))
    out_specs = P(spans, None)
    return jax.shard_map(make_local(dp_shape), mesh=fine, in_specs=in_specs, out_specs=out_specs, check_vma=False)
```

time: 76.8 us -> 74.6 us (0.971)
  local copies, waits for them, and re-layouts: 1.4 us -> 0.01 us
  blocking collectives: 68.3 us -> 67.3 us
    reshape x1 -> x0, local copies, waits for them, and re-layouts: 1.39 us -> none  [local(): norm_gain.reshape(1, features)]
    all_to_all x1, blocking collectives: 33.3 us -> 32.4 us  [local(): received = lax.all_to_all(contrib, ('c', 'xh', 'z'), 0, 0, tiled=True)]
where the time goes in v4:
time: 74.6 us; the launch traced here: 74.3 us
  blocking collectives  67.3 us (90%)
  Pallas kernels  3.88 us (5%)
  other arithmetic  1.94 us (3%)
  matrix products  1.12 us (2%)
    psum x4, blocking collectives, fsdp_sum(): return lax.psum(lax.psum(x, 'y'), 'xl')  35 us
    all_to_all x1, blocking collectives, local(): received = lax.all_to_all(contrib, ('c', 'xh', 'z'), 0, 0, tiled=True)  32.4 us
    pallas_call x1, Pallas kernels, local(): pl.pallas_call(functools.partial(pool_kernel, dp_shape), out_shape=jax.Sh...  2.48 us
    reduce_sum x1, other arithmetic, local(): partial_squares = jnp.sum(values * values, axis=-1)  1.81 us

profile of v4, /device:TPU:8, one launch (start us, length us, event | category | flops | bytes accessed | tf_op | source)
XLA Modules:
  0.0 74.3 jit_solution(12647606008283670812)
XLA Ops:
  0.0 0.0 copy-start
  0.0 0.0 copy-start.1
  0.0 1.8 %multiply_reduce_fusion = f32[2,512]{1,0:T(2,128)S(1)} fusion(bf16[2,512,640]{2,1,0:T(8,128)(2,1)} %states_ref.1), kind=kLoop, calls=%fused_computation | loop fusion | flops 1965056 | bytes 1314816 | tf_op jit(solution)/shard_map/reduce_sum | solution.py:64
  1.8 13.6 %psum.28 = f32[2,512]{1,0:T(2,128)S(1)} all-reduce(f32[2,512]{1,0:T(2,128)S(1)} %multiply_reduce_fusion), channel_id=1, replica_groups=mesh['z'=16,'xh'=2,'c'=2,'xl'=2,'y'=4] {'y'}, use_global_device_ids=true, to_apply=%region_1.0 | all-reduce | flops 1024 | bytes 8192 | tf_op jit(solution)/shard_map/psum | solution.py:34
  15.4 5.5 %psum.29.squares_ref = f32[2,512]{1,0:T(2,128)} all-reduce(f32[2,512]{1,0:T(2,128)S(1)} %psum.28), channel_id=1, replica_groups=mesh['z'=16,'xh'=2,'c'=2,'xl'=2,'y'=4] {'xl'}, use_global_device_ids=true, to_apply=%region_2.0 | all-reduce | flops 1024 | bytes 8192 | tf_op jit(solution)/shard_map/psum | solution.py:34
  20.9 2.5 %shard_map.55 = f32[64,1,640]{2,1,0:T(1,128)} custom-call(s32[2]{0:T(128)} %counts_ref.1, s32[128]{0:T(128)} %ids_ref.1, bf16[2,512,640]{2,1,0:T(8,128)(2,1)} %states_ref.1, f32[2,512]{1,0:T(2,128)} %psum.29.squares_ref), custom_call_target="tpu_custom_call" | custom-call | tf_op jit(solution)/shard_map/pallas_call | solution.py:71
  23.4 32.4 %all_to_all.5 = f32[64,1,640]{2,1,0:T(1,128)S(1)} all-to-all(f32[64,1,640]{2,1,0:T(1,128)} %shard_map.55), channel_id=1, replica_groups=mesh['z'=16,'xh'=2,'c'=2,'xl'=2,'y'=4] {'c','xh','z'}, dimensions={0} | all-to-all | bytes 327680 | tf_op jit(solution)/shard_map/all_to_all | solution.py:77
  55.7 0.1 reduce_sum.19
  55.9 0.0 copy-done.1
  55.9 0.0 copy-done
  55.9 1.1 %fusion = f32[1,2048]{1,0:T(1,128)S(1)} fusion(f32[640,1]{0,1:T(1,128)S(1)} %reshape.7, bf16[640,2048]{1,0:T(8,128)(2,1)S(1)} %copy-done), kind=kOutput, calls=%fused_computation.2 | convolution fusion | flops 15728640 | bytes 2632192 | tf_op jit(solution)/shard_map/dot_general | solution.py:80
  57.0 10.3 %psum.30 = f32[1,2048]{1,0:T(1,128)S(1)} all-reduce(f32[1,2048]{1,0:T(1,128)S(1)} %fusion), channel_id=1, replica_groups=mesh['z'=16,'xh'=2,'c'=2,'xl'=2,'y'=4] {'y'}, use_global_device_ids=true, to_apply=%region_4.0 | all-reduce | flops 2048 | bytes 16384 | tf_op jit(solution)/shard_map/psum | solution.py:34
  67.3 5.6 %psum.31.x_ref = f32[1,2048]{1,0:T(1,128)} all-reduce(f32[1,2048]{1,0:T(1,128)S(1)} %psum.30), channel_id=1, replica_groups=mesh['z'=16,'xh'=2,'c'=2,'xl'=2,'y'=4] {'xl'}, use_global_device_ids=true, to_apply=%region_5.0 | all-reduce | flops 2048 | bytes 16384 | tf_op jit(solution)/shard_map/psum | solution.py:34
  72.9 1.4 %shard_map.56 = f32[1,3840]{1,0:T(1,128)} custom-call(f32[1,2048]{1,0:T(1,128)} %psum.31.x_ref), custom_call_target="tpu_custom_call" | custom-call | tf_op jit(solution)/shard_map/pallas_call | solution.py:30
  (2 shorter events, 0.0 us)
Async XLA Ops:
  0.0 55.9 %copy-start = (bf16[640,2048]{1,0:T(8,128)(2,1)S(1)}, bf16[640,2048]{1,0:T(8,128)(2,1)}, u32[]{:S(2)}) copy-start(bf16[640,2048]{1,0:T(8,128)(2,1)} %param.9) | copy-start | bytes 7864324
  0.0 55.8 %copy-start.1 = (bf16[640]{0:T(1024)(128)(2,1)S(1)}, bf16[640]{0:T(1024)(128)(2,1)}, u32[]{:S(2)}) copy-start(bf16[640]{0:T(1024)(128)(2,1)} %param.8) | copy-start | bytes 3844

commit v5 on v4

--- a/solution.py
+++ b/solution.py
@@ -56,14 +56,23 @@
         out_ref[pl.ds(row, 1)] += pooled[None]
 
 
+def squares_kernel(states_ref, out_ref):
+    spans, slots_n, _ = states_ref.shape
+    for c in range(spans):
+        values = states_ref[c].astype(jnp.float32)
+        column = jnp.sum(values * values, axis=1, keepdims=True)
+        out_ref[pl.ds(c, 1), :] = jnp.transpose(jnp.broadcast_to(column, (slots_n, 128)))[:1, :]
+
+
 def make_local(dp_shape):
     groups = dp_shape[0] * dp_shape[1] * dp_shape[2]
 
     def local(states, valid_counts, section_ids, norm_gain, head_weight):
-        values = states.astype(jnp.float32)
-        partial_squares = jnp.sum(values * values, axis=-1)
+        local_spans, slots_n, features = states.shape
+        partial_squares = pl.pallas_call(
+            squares_kernel, out_shape=jax.ShapeDtypeStruct((local_spans, slots_n), jnp.float32)
+        )(states)
         squares = fsdp_sum(partial_squares)
-        local_spans, _, features = states.shape
         sec_local = local_spans // 2
         total_sections = sec_local * groups
         smem = pl.BlockSpec(memory_space=pltpu.SMEM)

time: 74.6 us -> 75.4 us (1.011)
  Pallas kernels: 3.88 us -> 6.39 us
  other arithmetic: 1.94 us -> 0.13 us
    pallas_call x0 -> x1, Pallas kernels: none -> 2.51 us  [local(): pl.pallas_call(squares_kernel, out_shape=jax.ShapeDtypeStruct((local_span...]
    reduce_sum x1 -> x0, other arithmetic: 1.81 us -> none  [local(): partial_squares = jnp.sum(values * values, axis=-1)]
where the time goes in v5:
time: 75.4 us; the launch traced here: 75.1 us
  blocking collectives  67.4 us (89%)
  Pallas kernels  6.39 us (8%)
  matrix products  1.12 us (1%)
    psum x4, blocking collectives, fsdp_sum(): return lax.psum(lax.psum(x, 'y'), 'xl')  35.1 us
    all_to_all x1, blocking collectives, local(): received = lax.all_to_all(contrib, ('c', 'xh', 'z'), 0, 0, tiled=True)  32.4 us
    pallas_call x1, Pallas kernels, local(): pl.pallas_call(squares_kernel, out_shape=jax.ShapeDtypeStruct((local_span...  2.51 us
    pallas_call x1, Pallas kernels, local(): pl.pallas_call(functools.partial(pool_kernel, dp_shape), out_shape=jax.Sh...  2.48 us

profile of v5, /device:TPU:8, one launch (start us, length us, event | category | flops | bytes accessed | tf_op | source)
XLA Modules:
  0.0 75.1 jit_solution(4924571703481986327)
XLA Ops:
  0.0 0.0 copy-start
  0.0 0.0 copy-start.1
  0.0 2.5 %shard_map.55 = f32[2,512]{1,0:T(2,128)} custom-call(bf16[2,512,640]{2,1,0:T(8,128)(2,1)} %states_ref.3), custom_call_target="tpu_custom_call" | custom-call | tf_op jit(solution)/shard_map/pallas_call | solution.py:72
  2.5 13.6 %psum.28 = f32[2,512]{1,0:T(2,128)S(1)} all-reduce(f32[2,512]{1,0:T(2,128)} %shard_map.55), channel_id=1, replica_groups=mesh['z'=16,'xh'=2,'c'=2,'xl'=2,'y'=4] {'y'}, use_global_device_ids=true, to_apply=%region_0.0 | all-reduce | flops 1024 | bytes 8192 | tf_op jit(solution)/shard_map/psum | solution.py:34
  16.2 5.5 %psum.29.squares_ref = f32[2,512]{1,0:T(2,128)} all-reduce(f32[2,512]{1,0:T(2,128)S(1)} %psum.28), channel_id=1, replica_groups=mesh['z'=16,'xh'=2,'c'=2,'xl'=2,'y'=4] {'xl'}, use_global_device_ids=true, to_apply=%region_1.0 | all-reduce | flops 1024 | bytes 8192 | tf_op jit(solution)/shard_map/psum | solution.py:34
  21.7 2.5 %shard_map.56 = f32[64,1,640]{2,1,0:T(1,128)} custom-call(s32[2]{0:T(128)} %counts_ref.1, s32[128]{0:T(128)} %ids_ref.1, bf16[2,512,640]{2,1,0:T(8,128)(2,1)} %states_ref.3, f32[2,512]{1,0:T(2,128)} %psum.29.squares_ref), custom_call_target="tpu_custom_call" | custom-call | tf_op jit(solution)/shard_map/pallas_call | solution.py:80
  24.2 32.4 %all_to_all.5 = f32[64,1,640]{2,1,0:T(1,128)S(1)} all-to-all(f32[64,1,640]{2,1,0:T(1,128)} %shard_map.56), channel_id=1, replica_groups=mesh['z'=16,'xh'=2,'c'=2,'xl'=2,'y'=4] {'c','xh','z'}, dimensions={0} | all-to-all | bytes 327680 | tf_op jit(solution)/shard_map/all_to_all | solution.py:86
  56.5 0.1 reduce_sum.9
  56.6 0.0 copy-done.1
  56.7 0.0 copy-done
  56.7 1.1 %fusion = f32[1,2048]{1,0:T(1,128)S(1)} fusion(f32[640,1]{0,1:T(1,128)S(1)} %reshape.7, bf16[640,2048]{1,0:T(8,128)(2,1)S(1)} %copy-done), kind=kOutput, calls=%fused_computation.1 | convolution fusion | flops 15728640 | bytes 2632192 | tf_op jit(solution)/shard_map/dot_general | solution.py:89
  57.8 10.3 %psum.30 = f32[1,2048]{1,0:T(1,128)S(1)} all-reduce(f32[1,2048]{1,0:T(1,128)S(1)} %fusion), channel_id=1, replica_groups=mesh['z'=16,'xh'=2,'c'=2,'xl'=2,'y'=4] {'y'}, use_global_device_ids=true, to_apply=%region_3.0 | all-reduce | flops 2048 | bytes 16384 | tf_op jit(solution)/shard_map/psum | solution.py:34
  68.1 5.6 %psum.31.x_ref = f32[1,2048]{1,0:T(1,128)} all-reduce(f32[1,2048]{1,0:T(1,128)S(1)} %psum.30), channel_id=1, replica_groups=mesh['z'=16,'xh'=2,'c'=2,'xl'=2,'y'=4] {'xl'}, use_global_device_ids=true, to_apply=%region_4.0 | all-reduce | flops 2048 | bytes 16384 | tf_op jit(solution)/shard_map/psum | solution.py:34
  73.7 1.4 %shard_map.57 = f32[1,3840]{1,0:T(1,128)} custom-call(f32[1,2048]{1,0:T(1,128)} %psum.31.x_ref), custom_call_target="tpu_custom_call" | custom-call | tf_op jit(solution)/shard_map/pallas_call | solution.py:30
  (2 shorter events, 0.0 us)
Async XLA Ops:
  0.0 56.7 %copy-start = (bf16[640,2048]{1,0:T(8,128)(2,1)S(1)}, bf16[640,2048]{1,0:T(8,128)(2,1)}, u32[]{:S(2)}) copy-start(bf16[640,2048]{1,0:T(8,128)(2,1)} %param.9) | copy-start | bytes 7864324
  0.0 56.6 %copy-start.1 = (bf16[640]{0:T(1024)(128)(2,1)S(1)}, bf16[640]{0:T(1024)(128)(2,1)}, u32[]{:S(2)}) copy-start(bf16[640]{0:T(1024)(128)(2,1)} %param.8) | copy-start | bytes 3844

commit v6 on v4

--- a/solution.py
+++ b/solution.py
@@ -40,14 +40,20 @@
     sec_local = out_ref.shape[0] // (z_n * xh_n * c_n)
     me = (lax.axis_index("z") * xh_n + lax.axis_index("xh")) * c_n + lax.axis_index("c")
     out_ref[...] = jnp.zeros(out_ref.shape, jnp.float32)
+    rows = lax.broadcasted_iota(jnp.int32, (8, slots_n), 0)
     for c in range(spans):
         count = counts_ref[c]
         scale = lax.rsqrt(squares_ref[pl.ds(c, 1), :] / D + epsilon)
         slots = lax.broadcasted_iota(jnp.int32, scale.shape, 1)
         weights = jnp.where(slots < count, scale, 0.0)
-        column = jnp.transpose(jnp.broadcast_to(weights, (128, slots_n)))[:, :1]
-        values = states_ref[c].astype(jnp.float32)
-        sums = jnp.sum(values * column, axis=0, keepdims=True)
+        high = weights.astype(jnp.bfloat16)
+        rest = weights - high.astype(jnp.float32)
+        middle = rest.astype(jnp.bfloat16)
+        low = (rest - middle.astype(jnp.float32)).astype(jnp.bfloat16)
+        zero = jnp.zeros_like(high)
+        parts = jnp.where(rows == 0, high, jnp.where(rows == 1, middle, jnp.where(rows == 2, low, zero)))
+        partial = jnp.dot(parts, states_ref[c], preferred_element_type=jnp.float32)
+        sums = partial[0:1, :] + partial[1:2, :] + partial[2:3, :]
         pooled = sums / count.astype(jnp.float32)
         section = ids_ref[me * spans + c]
         owner = section // sec_local

time: 74.6 us -> 74.4 us (level)
  no operation moved by 1% of the time
where the time goes in v6:
time: 74.4 us; the launch traced here: 74.1 us
  blocking collectives  67.3 us (90%)
  Pallas kernels  3.67 us (5%)
  other arithmetic  1.94 us (3%)
  matrix products  1.12 us (2%)
    psum x4, blocking collectives, fsdp_sum(): return lax.psum(lax.psum(x, 'y'), 'xl')  35 us
    all_to_all x1, blocking collectives, local(): received = lax.all_to_all(contrib, ('c', 'xh', 'z'), 0, 0, tiled=True)  32.4 us
    pallas_call x1, Pallas kernels, local(): pl.pallas_call(functools.partial(pool_kernel, dp_shape), out_shape=jax.Sh...  2.27 us
    reduce_sum x1, other arithmetic, local(): partial_squares = jnp.sum(values * values, axis=-1)  1.81 us

profile of v6, /device:TPU:8, one launch (start us, length us, event | category | flops | bytes accessed | tf_op | source)
XLA Modules:
  0.0 74.1 jit_solution(7690335787819504338)
XLA Ops:
  0.0 0.0 copy-start
  0.0 0.0 copy-start.1
  0.0 1.8 %multiply_reduce_fusion = f32[2,512]{1,0:T(2,128)S(1)} fusion(bf16[2,512,640]{2,1,0:T(8,128)(2,1)} %states_ref.1), kind=kLoop, calls=%fused_computation | loop fusion | flops 1965056 | bytes 1314816 | tf_op jit(solution)/shard_map/reduce_sum | solution.py:70
  1.8 13.6 %psum.28 = f32[2,512]{1,0:T(2,128)S(1)} all-reduce(f32[2,512]{1,0:T(2,128)S(1)} %multiply_reduce_fusion), channel_id=1, replica_groups=mesh['z'=16,'xh'=2,'c'=2,'xl'=2,'y'=4] {'y'}, use_global_device_ids=true, to_apply=%region_1.0 | all-reduce | flops 1024 | bytes 8192 | tf_op jit(solution)/shard_map/psum | solution.py:34
  15.4 5.5 %psum.29.squares_ref = f32[2,512]{1,0:T(2,128)} all-reduce(f32[2,512]{1,0:T(2,128)S(1)} %psum.28), channel_id=1, replica_groups=mesh['z'=16,'xh'=2,'c'=2,'xl'=2,'y'=4] {'xl'}, use_global_device_ids=true, to_apply=%region_2.0 | all-reduce | flops 1024 | bytes 8192 | tf_op jit(solution)/shard_map/psum | solution.py:34
  20.9 2.3 %shard_map.55 = f32[64,1,640]{2,1,0:T(1,128)} custom-call(s32[2]{0:T(128)} %counts_ref.1, s32[128]{0:T(128)} %ids_ref.1, bf16[2,512,640]{2,1,0:T(8,128)(2,1)} %states_ref.1, f32[2,512]{1,0:T(2,128)} %psum.29.squares_ref), custom_call_target="tpu_custom_call" | custom-call | tf_op jit(solution)/shard_map/pallas_call | solution.py:77
  23.2 32.4 %all_to_all.5 = f32[64,1,640]{2,1,0:T(1,128)S(1)} all-to-all(f32[64,1,640]{2,1,0:T(1,128)} %shard_map.55), channel_id=1, replica_groups=mesh['z'=16,'xh'=2,'c'=2,'xl'=2,'y'=4] {'c','xh','z'}, dimensions={0} | all-to-all | bytes 327680 | tf_op jit(solution)/shard_map/all_to_all | solution.py:83
  55.5 0.1 reduce_sum.19
  55.6 0.0 copy-done.1
  55.7 0.0 copy-done
  55.7 1.1 %fusion = f32[1,2048]{1,0:T(1,128)S(1)} fusion(f32[640,1]{0,1:T(1,128)S(1)} %reshape.7, bf16[640,2048]{1,0:T(8,128)(2,1)S(1)} %copy-done), kind=kOutput, calls=%fused_computation.2 | convolution fusion | flops 15728640 | bytes 2632192 | tf_op jit(solution)/shard_map/dot_general | solution.py:86
  56.8 10.3 %psum.30 = f32[1,2048]{1,0:T(1,128)S(1)} all-reduce(f32[1,2048]{1,0:T(1,128)S(1)} %fusion), channel_id=1, replica_groups=mesh['z'=16,'xh'=2,'c'=2,'xl'=2,'y'=4] {'y'}, use_global_device_ids=true, to_apply=%region_4.0 | all-reduce | flops 2048 | bytes 16384 | tf_op jit(solution)/shard_map/psum | solution.py:34
  67.1 5.6 %psum.31.x_ref = f32[1,2048]{1,0:T(1,128)} all-reduce(f32[1,2048]{1,0:T(1,128)S(1)} %psum.30), channel_id=1, replica_groups=mesh['z'=16,'xh'=2,'c'=2,'xl'=2,'y'=4] {'xl'}, use_global_device_ids=true, to_apply=%region_5.0 | all-reduce | flops 2048 | bytes 16384 | tf_op jit(solution)/shard_map/psum | solution.py:34
  72.7 1.4 %shard_map.56 = f32[1,3840]{1,0:T(1,128)} custom-call(f32[1,2048]{1,0:T(1,128)} %psum.31.x_ref), custom_call_target="tpu_custom_call" | custom-call | tf_op jit(solution)/shard_map/pallas_call | solution.py:30
  (2 shorter events, 0.0 us)
Async XLA Ops:
  0.0 55.7 %copy-start = (bf16[640,2048]{1,0:T(8,128)(2,1)S(1)}, bf16[640,2048]{1,0:T(8,128)(2,1)}, u32[]{:S(2)}) copy-start(bf16[640,2048]{1,0:T(8,128)(2,1)} %param.9) | copy-start | bytes 7864324
  0.0 55.6 %copy-start.1 = (bf16[640]{0:T(1024)(128)(2,1)S(1)}, bf16[640]{0:T(1024)(128)(2,1)}, u32[]{:S(2)}) copy-start(bf16[640]{0:T(1024)(128)(2,1)} %param.8) | copy-start | bytes 3844

commit v7 on v4

--- a/solution.py
+++ b/solution.py
@@ -35,25 +35,47 @@
 
 
 def pool_kernel(dp_shape, counts_ref, ids_ref, states_ref, squares_ref, out_ref):
-    spans, slots_n, _ = states_ref.shape
+    _, slots_n, _ = states_ref.shape
+    spans = squares_ref.shape[0]
     z_n, xh_n, c_n = dp_shape
     sec_local = out_ref.shape[0] // (z_n * xh_n * c_n)
     me = (lax.axis_index("z") * xh_n + lax.axis_index("xh")) * c_n + lax.axis_index("c")
-    out_ref[...] = jnp.zeros(out_ref.shape, jnp.float32)
-    for c in range(spans):
-        count = counts_ref[c]
-        scale = lax.rsqrt(squares_ref[pl.ds(c, 1), :] / D + epsilon)
-        slots = lax.broadcasted_iota(jnp.int32, scale.shape, 1)
-        weights = jnp.where(slots < count, scale, 0.0)
-        column = jnp.transpose(jnp.broadcast_to(weights, (128, slots_n)))[:, :1]
-        values = states_ref[c].astype(jnp.float32)
-        sums = jnp.sum(values * column, axis=0, keepdims=True)
-        pooled = sums / count.astype(jnp.float32)
-        section = ids_ref[me * spans + c]
-        owner = section // sec_local
-        place = ((owner % c_n) * xh_n + (owner // c_n) % xh_n) * z_n + owner // (c_n * xh_n)
-        row = place * sec_local + section % sec_local
-        out_ref[pl.ds(row, 1)] += pooled[None]
+    c = pl.program_id(0)
+
+    @pl.when(c == 0)
+    def _():
+        out_ref[...] = jnp.zeros(out_ref.shape, jnp.float32)
+
+    rows = lax.broadcasted_iota(jnp.int32, (8, slots_n), 0)
+    count = counts_ref[c]
+    scale = lax.rsqrt(squares_ref[pl.ds(c, 1), :] / D + epsilon)
+    slots = lax.broadcasted_iota(jnp.int32, scale.shape, 1)
+    weights = jnp.where(slots < count, scale, 0.0)
+    parts = jnp.where(rows < 3, split3(weights, rows), jnp.zeros((8, slots_n), jnp.bfloat16))
+    partial = jnp.dot(parts, states_ref[0], preferred_element_type=jnp.float32)
+    sums = partial[0:1, :] + partial[1:2, :] + partial[2:3, :]
+    pooled = sums / count.astype(jnp.float32)
+    section = ids_ref[me * spans + c]
+    owner = section // sec_local
+    place = ((owner % c_n) * xh_n + (owner // c_n) % xh_n) * z_n + owner // (c_n * xh_n)
+    row = place * sec_local + section % sec_local
+    out_ref[pl.ds(row, 1)] += pooled[None]
+
+
+def split3(x, rows):
+    high = x.astype(jnp.bfloat16)
+    rest = x - high.astype(jnp.float32)
+    middle = rest.astype(jnp.bfloat16)
+    low = (rest - middle.astype(jnp.float32)).astype(jnp.bfloat16)
+    return jnp.where(rows == 0, high, jnp.where(rows == 1, middle, low))
+
+
+def split3_rounded(x):
+    high = lax.reduce_precision(x, exponent_bits=8, mantissa_bits=7)
+    rest = x - high
+    middle = lax.reduce_precision(rest, exponent_bits=8, mantissa_bits=7)
+    low = rest - middle
+    return jnp.stack([high, middle, low]).astype(jnp.bfloat16)
 
 
 def make_local(dp_shape):
@@ -63,7 +85,7 @@
         values = states.astype(jnp.float32)
         partial_squares = jnp.sum(values * values, axis=-1)
         squares = fsdp_sum(partial_squares)
-        local_spans, _, features = states.shape
+        local_spans, slots_n, features = states.shape
         sec_local = local_spans // 2
         total_sections = sec_local * groups
         smem = pl.BlockSpec(memory_space=pltpu.SMEM)
@@ -71,13 +93,21 @@
         contrib = pl.pallas_call(
             functools.partial(pool_kernel, dp_shape),
             out_shape=jax.ShapeDtypeStruct((total_sections, 1, features), jnp.float32),
-            in_specs=[smem, smem, vmem, vmem],
-            out_specs=vmem,
+            grid=(local_spans,),
+            in_specs=[
+                smem,
+                smem,
+                pl.BlockSpec((1, slots_n, features), lambda c: (c, 0, 0)),
+                pl.BlockSpec((local_spans, slots_n), lambda c: (0, 0)),
+            ],
+            out_specs=pl.BlockSpec((total_sections, 1, features), lambda c: (0, 0, 0)),
         )(valid_counts, section_ids, states, squares)
         received = lax.all_to_all(contrib, ("c", "xh", "z"), 0, 0, tiled=True)
         section_sums = jnp.sum(received.reshape(groups, sec_local, features), axis=0)
         section_sums = section_sums * norm_gain.astype(jnp.float32)[None, :]
-        terms = jnp.dot(section_sums, head_weight.astype(jnp.float32), precision=lax.Precision.HIGHEST)
+        parts = split3_rounded(section_sums)
+        stacked = jnp.dot(parts.reshape(-1, features), head_weight, preferred_element_type=jnp.float32)
+        terms = jnp.sum(stacked.reshape(3, sec_local, -1), axis=0)
         projected = fsdp_sum(terms)
         return nested(projected)
 

time: 74.6 us -> 73.7 us (0.988)
  no operation moved by 1% of the time
where the time goes in v7:
time: 73.7 us; the launch traced here: 73.5 us
  blocking collectives  67.3 us (91%)
  Pallas kernels  3.62 us (5%)
  other arithmetic  1.95 us (3%)
    psum x4, blocking collectives, fsdp_sum(): return lax.psum(lax.psum(x, 'y'), 'xl')  35 us
    all_to_all x1, blocking collectives, local(): received = lax.all_to_all(contrib, ('c', 'xh', 'z'), 0, 0, tiled=True)  32.4 us
    pallas_call x1, Pallas kernels, local(): pl.pallas_call(functools.partial(pool_kernel, dp_shape), out_shape=jax.Sh...  2.22 us
    reduce_sum x1, other arithmetic, local(): partial_squares = jnp.sum(values * values, axis=-1)  1.81 us

profile of v7, /device:TPU:8, one launch (start us, length us, event | category | flops | bytes accessed | tf_op | source)
XLA Modules:
  0.0 73.5 jit_solution(140871572246136392)
XLA Ops:
  0.0 0.0 copy-start
  0.0 0.0 copy-start.1
  0.0 1.8 %multiply_reduce_fusion = f32[2,512]{1,0:T(2,128)S(1)} fusion(bf16[2,512,640]{2,1,0:T(8,128)(2,1)} %states_ref.1), kind=kLoop, calls=%fused_computation | loop fusion | flops 1965056 | bytes 1314816 | tf_op jit(solution)/shard_map/reduce_sum | solution.py:86
  1.8 13.6 %psum.28 = f32[2,512]{1,0:T(2,128)S(1)} all-reduce(f32[2,512]{1,0:T(2,128)S(1)} %multiply_reduce_fusion), channel_id=1, replica_groups=mesh['z'=16,'xh'=2,'c'=2,'xl'=2,'y'=4] {'y'}, use_global_device_ids=true, to_apply=%region_1.0 | all-reduce | flops 1024 | bytes 8192 | tf_op jit(solution)/shard_map/psum | solution.py:34
  15.4 5.5 %psum.29.squares_ref = f32[2,512]{1,0:T(2,128)} all-reduce(f32[2,512]{1,0:T(2,128)S(1)} %psum.28), channel_id=1, replica_groups=mesh['z'=16,'xh'=2,'c'=2,'xl'=2,'y'=4] {'xl'}, use_global_device_ids=true, to_apply=%region_2.0 | all-reduce | flops 1024 | bytes 8192 | tf_op jit(solution)/shard_map/psum | solution.py:34
  20.9 2.2 %shard_map.55 = f32[64,1,640]{2,1,0:T(1,128)} custom-call(s32[2]{0:T(128)} %counts_ref.1, s32[128]{0:T(128)} %ids_ref.1, bf16[2,512,640]{2,1,0:T(8,128)(2,1)} %states_ref.1, f32[2,512]{1,0:T(2,128)} %psum.29.squares_ref), custom_call_target="tpu_custom_call" | custom-call | tf_op jit(solution)/shard_map/pallas_call | solution.py:93
  23.1 32.4 %all_to_all.5 = f32[64,1,640]{2,1,0:T(1,128)S(1)} all-to-all(f32[64,1,640]{2,1,0:T(1,128)} %shard_map.55), channel_id=1, replica_groups=mesh['z'=16,'xh'=2,'c'=2,'xl'=2,'y'=4] {'c','xh','z'}, dimensions={0} | all-to-all | bytes 327680 | tf_op jit(solution)/shard_map/all_to_all | solution.py:105
  55.5 0.1 reduce_sum.30
  55.6 0.0 copy-done.1
  55.6 0.0 copy-done
  55.7 0.5 convolution_reduce_fusion
  56.1 10.3 %psum.30 = f32[1,2048]{1,0:T(1,128)S(1)} all-reduce(f32[1,2048]{1,0:T(1,128)S(1)} %bitcast.2), channel_id=1, replica_groups=mesh['z'=16,'xh'=2,'c'=2,'xl'=2,'y'=4] {'y'}, use_global_device_ids=true, to_apply=%region_5.0 | all-reduce | flops 2048 | bytes 16384 | tf_op jit(solution)/shard_map/psum | solution.py:34
  66.5 5.6 %psum.31.x_ref = f32[1,2048]{1,0:T(1,128)} all-reduce(f32[1,2048]{1,0:T(1,128)S(1)} %psum.30), channel_id=1, replica_groups=mesh['z'=16,'xh'=2,'c'=2,'xl'=2,'y'=4] {'xl'}, use_global_device_ids=true, to_apply=%region_6.0 | all-reduce | flops 2048 | bytes 16384 | tf_op jit(solution)/shard_map/psum | solution.py:34
  72.1 1.4 %shard_map.56 = f32[1,3840]{1,0:T(1,128)} custom-call(f32[1,2048]{1,0:T(1,128)} %psum.31.x_ref), custom_call_target="tpu_custom_call" | custom-call | tf_op jit(solution)/shard_map/pallas_call | solution.py:30
  (4 shorter events, 0.0 us)
Async XLA Ops:
  0.0 55.6 %copy-start = (bf16[640,2048]{1,0:T(8,128)(2,1)S(1)}, bf16[640,2048]{1,0:T(8,128)(2,1)}, u32[]{:S(2)}) copy-start(bf16[640,2048]{1,0:T(8,128)(2,1)} %param.9) | copy-start | bytes 7864324
  0.0 55.6 %copy-start.1 = (bf16[640]{0:T(1024)(128)(2,1)S(1)}, bf16[640]{0:T(1024)(128)(2,1)}, u32[]{:S(2)}) copy-start(bf16[640]{0:T(1024)(128)(2,1)} %param.8) | copy-start | bytes 3844

commit v8 on v7

--- a/solution.py
+++ b/solution.py
@@ -27,7 +27,10 @@
 def nested(projected):
     rows, width = projected.shape
     out = jax.ShapeDtypeStruct((rows, width // 8 + width // 4 + width // 2 + width), jnp.float32)
-    return pl.pallas_call(nested_kernel, out_shape=out)(projected)
+    vmem = pl.BlockSpec(memory_space=pltpu.VMEM)
+    return pl.pallas_call(nested_kernel, out_shape=out, in_specs=[vmem])(
+        pltpu.with_memory_space_constraint(projected, pltpu.VMEM)
+    )
 
 
 def fsdp_sum(x):
@@ -98,10 +101,10 @@
                 smem,
                 smem,
                 pl.BlockSpec((1, slots_n, features), lambda c: (c, 0, 0)),
-                pl.BlockSpec((local_spans, slots_n), lambda c: (0, 0)),
+                pl.BlockSpec((local_spans, slots_n), lambda c: (0, 0), memory_space=pltpu.VMEM),
             ],
             out_specs=pl.BlockSpec((total_sections, 1, features), lambda c: (0, 0, 0)),
-        )(valid_counts, section_ids, states, squares)
+        )(valid_counts, section_ids, states, pltpu.with_memory_space_constraint(squares, pltpu.VMEM))
         received = lax.all_to_all(contrib, ("c", "xh", "z"), 0, 0, tiled=True)
         section_sums = jnp.sum(received.reshape(groups, sec_local, features), axis=0)
         section_sums = section_sums * norm_gain.astype(jnp.float32)[None, :]

time: 73.7 us -> 71.8 us (0.974)
  blocking collectives: 67.3 us -> 66.2 us
    psum x4, blocking collectives: 35 us -> 33.8 us  [fsdp_sum(): return lax.psum(lax.psum(x, 'y'), 'xl')]
where the time goes in v8:
time: 71.8 us; the launch traced here: 71.6 us
  blocking collectives  66.2 us (92%)
  Pallas kernels  2.92 us (4%)
  other arithmetic  1.95 us (3%)
    psum x4, blocking collectives, fsdp_sum(): return lax.psum(lax.psum(x, 'y'), 'xl')  33.8 us
    all_to_all x1, blocking collectives, local(): received = lax.all_to_all(contrib, ('c', 'xh', 'z'), 0, 0, tiled=True)  32.4 us
    pallas_call x1, Pallas kernels, local(): pl.pallas_call(functools.partial(pool_kernel, dp_shape), out_shape=jax.Sh...  2.21 us
    reduce_sum x1, other arithmetic, local(): partial_squares = jnp.sum(values * values, axis=-1)  1.81 us

profile of v8, /device:TPU:8, one launch (start us, length us, event | category | flops | bytes accessed | tf_op | source)
XLA Modules:
  0.0 71.6 jit_solution(4297189926865712992)
XLA Ops:
  0.0 0.0 copy-start
  0.0 0.0 copy-start.1
  0.0 1.8 %multiply_reduce_fusion = f32[2,512]{1,0:T(2,128)S(1)} fusion(bf16[2,512,640]{2,1,0:T(8,128)(2,1)} %states_ref.1), kind=kLoop, calls=%fused_computation | loop fusion | flops 1965056 | bytes 1314816 | tf_op jit(solution)/shard_map/reduce_sum | solution.py:89
  1.8 13.6 %psum.28 = f32[2,512]{1,0:T(2,128)S(1)} all-reduce(f32[2,512]{1,0:T(2,128)S(1)} %multiply_reduce_fusion), channel_id=1, replica_groups=mesh['z'=16,'xh'=2,'c'=2,'xl'=2,'y'=4] {'y'}, use_global_device_ids=true, to_apply=%region_1.0 | all-reduce | flops 1024 | bytes 8192 | tf_op jit(solution)/shard_map/psum | solution.py:37
  15.4 4.9 %psum.29.squares_ref = f32[2,512]{1,0:T(2,128)S(1)} all-reduce(f32[2,512]{1,0:T(2,128)S(1)} %psum.28), channel_id=1, replica_groups=mesh['z'=16,'xh'=2,'c'=2,'xl'=2,'y'=4] {'xl'}, use_global_device_ids=true, to_apply=%region_2.0 | all-reduce | flops 1024 | bytes 8192 | tf_op jit(solution)/shard_map/psum | solution.py:37
  20.3 2.2 %shard_map.55 = f32[64,1,640]{2,1,0:T(1,128)} custom-call(s32[2]{0:T(128)} %counts_ref.1, s32[128]{0:T(128)} %ids_ref.1, bf16[2,512,640]{2,1,0:T(8,128)(2,1)} %states_ref.1, f32[2,512]{1,0:T(2,128)S(1)} %psum.29.squares_ref), custom_call_target="tpu_custom_call" | custom-call | tf_op jit(solution)/shard_map/pallas_call | solution.py:96
  22.5 32.4 %all_to_all.5 = f32[64,1,640]{2,1,0:T(1,128)S(1)} all-to-all(f32[64,1,640]{2,1,0:T(1,128)} %shard_map.55), channel_id=1, replica_groups=mesh['z'=16,'xh'=2,'c'=2,'xl'=2,'y'=4] {'c','xh','z'}, dimensions={0} | all-to-all | bytes 327680 | tf_op jit(solution)/shard_map/all_to_all | solution.py:108
  54.9 0.1 reduce_sum.30
  55.0 0.0 copy-done.1
  55.1 0.0 copy-done
  55.1 0.5 convolution_reduce_fusion
  55.5 10.3 %psum.30 = f32[1,2048]{1,0:T(1,128)S(1)} all-reduce(f32[1,2048]{1,0:T(1,128)S(1)} %bitcast.2), channel_id=1, replica_groups=mesh['z'=16,'xh'=2,'c'=2,'xl'=2,'y'=4] {'y'}, use_global_device_ids=true, to_apply=%region_5.0 | all-reduce | flops 2048 | bytes 16384 | tf_op jit(solution)/shard_map/psum | solution.py:37
  65.9 5.0 %psum.31.x_ref = f32[1,2048]{1,0:T(1,128)S(1)} all-reduce(f32[1,2048]{1,0:T(1,128)S(1)} %psum.30), channel_id=1, replica_groups=mesh['z'=16,'xh'=2,'c'=2,'xl'=2,'y'=4] {'xl'}, use_global_device_ids=true, to_apply=%region_6.0 | all-reduce | flops 2048 | bytes 16384 | tf_op jit(solution)/shard_map/psum | solution.py:37
  70.9 0.7 shard_map.56
  (4 shorter events, 0.0 us)
Async XLA Ops:
  0.0 55.1 %copy-start = (bf16[640,2048]{1,0:T(8,128)(2,1)S(1)}, bf16[640,2048]{1,0:T(8,128)(2,1)}, u32[]{:S(2)}) copy-start(bf16[640,2048]{1,0:T(8,128)(2,1)} %param.9) | copy-start | bytes 7864324
  0.0 55.0 %copy-start.1 = (bf16[640]{0:T(1024)(128)(2,1)S(1)}, bf16[640]{0:T(1024)(128)(2,1)}, u32[]{:S(2)}) copy-start(bf16[640]{0:T(1024)(128)(2,1)} %param.8) | copy-start | bytes 3844

commit v9 on v8

--- a/solution.py
+++ b/solution.py
@@ -95,7 +95,7 @@
         vmem = pl.BlockSpec(memory_space=pltpu.VMEM)
         contrib = pl.pallas_call(
             functools.partial(pool_kernel, dp_shape),
-            out_shape=jax.ShapeDtypeStruct((total_sections, 1, features), jnp.float32),
+            out_shape=pltpu.VMEM((total_sections, 1, features), jnp.float32),
             grid=(local_spans,),
             in_specs=[
                 smem,
@@ -103,7 +103,7 @@
                 pl.BlockSpec((1, slots_n, features), lambda c: (c, 0, 0)),
                 pl.BlockSpec((local_spans, slots_n), lambda c: (0, 0), memory_space=pltpu.VMEM),
             ],
-            out_specs=pl.BlockSpec((total_sections, 1, features), lambda c: (0, 0, 0)),
+            out_specs=pl.BlockSpec((total_sections, 1, features), lambda c: (0, 0, 0), memory_space=pltpu.VMEM),
         )(valid_counts, section_ids, states, pltpu.with_memory_space_constraint(squares, pltpu.VMEM))
         received = lax.all_to_all(contrib, ("c", "xh", "z"), 0, 0, tiled=True)
         section_sums = jnp.sum(received.reshape(groups, sec_local, features), axis=0)

time: 71.8 us -> 71 us (0.989)
  no operation moved by 1% of the time
where the time goes in v9:
time: 71 us; the launch traced here: 70.7 us
  blocking collectives  66 us (93%)
  Pallas kernels  2.27 us (3%)
  other arithmetic  1.95 us (3%)
    psum x4, blocking collectives, fsdp_sum(): return lax.psum(lax.psum(x, 'y'), 'xl')  33.8 us
    all_to_all x1, blocking collectives, local(): received = lax.all_to_all(contrib, ('c', 'xh', 'z'), 0, 0, tiled=True)  32.2 us
    reduce_sum x1, other arithmetic, local(): partial_squares = jnp.sum(values * values, axis=-1)  1.81 us
    pallas_call x1, Pallas kernels, local(): pl.pallas_call(functools.partial(pool_kernel, dp_shape), out_shape=pltpu....  1.56 us

profile of v9, /device:TPU:8, one launch (start us, length us, event | category | flops | bytes accessed | tf_op | source)
XLA Modules:
  0.0 70.7 jit_solution(13016947049312298295)
XLA Ops:
  0.0 0.0 copy-start
  0.0 0.0 copy-start.1
  0.0 1.8 %multiply_reduce_fusion = f32[2,512]{1,0:T(2,128)S(1)} fusion(bf16[2,512,640]{2,1,0:T(8,128)(2,1)} %states_ref.1), kind=kLoop, calls=%fused_computation | loop fusion | flops 1965056 | bytes 1314816 | tf_op jit(solution)/shard_map/reduce_sum | solution.py:89
  1.8 13.6 %psum.28 = f32[2,512]{1,0:T(2,128)S(1)} all-reduce(f32[2,512]{1,0:T(2,128)S(1)} %multiply_reduce_fusion), channel_id=1, replica_groups=mesh['z'=16,'xh'=2,'c'=2,'xl'=2,'y'=4] {'y'}, use_global_device_ids=true, to_apply=%region_1.0 | all-reduce | flops 1024 | bytes 8192 | tf_op jit(solution)/shard_map/psum | solution.py:37
  15.4 4.9 %psum.29.squares_ref = f32[2,512]{1,0:T(2,128)S(1)} all-reduce(f32[2,512]{1,0:T(2,128)S(1)} %psum.28), channel_id=1, replica_groups=mesh['z'=16,'xh'=2,'c'=2,'xl'=2,'y'=4] {'xl'}, use_global_device_ids=true, to_apply=%region_2.0 | all-reduce | flops 1024 | bytes 8192 | tf_op jit(solution)/shard_map/psum | solution.py:37
  20.3 1.6 %shard_map.55 = f32[64,1,640]{2,1,0:T(1,128)S(1)} custom-call(s32[2]{0:T(128)} %counts_ref.1, s32[128]{0:T(128)} %ids_ref.1, bf16[2,512,640]{2,1,0:T(8,128)(2,1)} %states_ref.1, f32[2,512]{1,0:T(2,128)S(1)} %psum.29.squares_ref), custom_call_target="tpu_custom_call" | custom-call | tf_op jit(solution)/shard_map/pallas_call | solution.py:96
  21.9 32.2 %all_to_all.5 = f32[64,1,640]{2,1,0:T(1,128)S(1)} all-to-all(f32[64,1,640]{2,1,0:T(1,128)S(1)} %shard_map.55), channel_id=1, replica_groups=mesh['z'=16,'xh'=2,'c'=2,'xl'=2,'y'=4] {'c','xh','z'}, dimensions={0} | all-to-all | bytes 327680 | tf_op jit(solution)/shard_map/all_to_all | solution.py:108
  54.0 0.1 reduce_sum.30
  54.2 0.0 copy-done.1
  54.2 0.0 copy-done
  54.2 0.5 convolution_reduce_fusion
  54.7 10.3 %psum.30 = f32[1,2048]{1,0:T(1,128)S(1)} all-reduce(f32[1,2048]{1,0:T(1,128)S(1)} %bitcast.2), channel_id=1, replica_groups=mesh['z'=16,'xh'=2,'c'=2,'xl'=2,'y'=4] {'y'}, use_global_device_ids=true, to_apply=%region_5.0 | all-reduce | flops 2048 | bytes 16384 | tf_op jit(solution)/shard_map/psum | solution.py:37
  65.0 5.0 %psum.31.x_ref = f32[1,2048]{1,0:T(1,128)S(1)} all-reduce(f32[1,2048]{1,0:T(1,128)S(1)} %psum.30), channel_id=1, replica_groups=mesh['z'=16,'xh'=2,'c'=2,'xl'=2,'y'=4] {'xl'}, use_global_device_ids=true, to_apply=%region_6.0 | all-reduce | flops 2048 | bytes 16384 | tf_op jit(solution)/shard_map/psum | solution.py:37
  70.0 0.7 shard_map.56
  (4 shorter events, 0.0 us)
Async XLA Ops:
  0.0 54.2 %copy-start = (bf16[640,2048]{1,0:T(8,128)(2,1)S(1)}, bf16[640,2048]{1,0:T(8,128)(2,1)}, u32[]{:S(2)}) copy-start(bf16[640,2048]{1,0:T(8,128)(2,1)} %param.9) | copy-start | bytes 7864324
  0.0 54.2 %copy-start.1 = (bf16[640]{0:T(1024)(128)(2,1)S(1)}, bf16[640]{0:T(1024)(128)(2,1)}, u32[]{:S(2)}) copy-start(bf16[640]{0:T(1024)(128)(2,1)} %param.8) | copy-start | bytes 3844

commit v10 on v5

--- a/solution.py
+++ b/solution.py
@@ -27,7 +27,10 @@
 def nested(projected):
     rows, width = projected.shape
     out = jax.ShapeDtypeStruct((rows, width // 8 + width // 4 + width // 2 + width), jnp.float32)
-    return pl.pallas_call(nested_kernel, out_shape=out)(projected)
+    vmem = pl.BlockSpec(memory_space=pltpu.VMEM)
+    return pl.pallas_call(nested_kernel, out_shape=out, in_specs=[vmem])(
+        pltpu.with_memory_space_constraint(projected, pltpu.VMEM)
+    )
 
 
 def fsdp_sum(x):
@@ -40,14 +43,15 @@
     sec_local = out_ref.shape[0] // (z_n * xh_n * c_n)
     me = (lax.axis_index("z") * xh_n + lax.axis_index("xh")) * c_n + lax.axis_index("c")
     out_ref[...] = jnp.zeros(out_ref.shape, jnp.float32)
+    rows = lax.broadcasted_iota(jnp.int32, (8, slots_n), 0)
     for c in range(spans):
         count = counts_ref[c]
         scale = lax.rsqrt(squares_ref[pl.ds(c, 1), :] / D + epsilon)
         slots = lax.broadcasted_iota(jnp.int32, scale.shape, 1)
         weights = jnp.where(slots < count, scale, 0.0)
-        column = jnp.transpose(jnp.broadcast_to(weights, (128, slots_n)))[:, :1]
-        values = states_ref[c].astype(jnp.float32)
-        sums = jnp.sum(values * column, axis=0, keepdims=True)
+        parts = jnp.where(rows < 3, split3(weights, rows), jnp.zeros((8, slots_n), jnp.bfloat16))
+        partial = jnp.dot(parts, states_ref[c], preferred_element_type=jnp.float32)
+        sums = partial[0:1, :] + partial[1:2, :] + partial[2:3, :]
         pooled = sums / count.astype(jnp.float32)
         section = ids_ref[me * spans + c]
         owner = section // sec_local
@@ -56,12 +60,30 @@
         out_ref[pl.ds(row, 1)] += pooled[None]
 
 
-def squares_kernel(states_ref, out_ref):
+def split3(x, rows):
+    high = x.astype(jnp.bfloat16)
+    rest = x - high.astype(jnp.float32)
+    middle = rest.astype(jnp.bfloat16)
+    low = (rest - middle.astype(jnp.float32)).astype(jnp.bfloat16)
+    return jnp.where(rows == 0, high, jnp.where(rows == 1, middle, low))
+
+
+def split3_rounded(x):
+    high = lax.reduce_precision(x, exponent_bits=8, mantissa_bits=7)
+    rest = x - high
+    middle = lax.reduce_precision(rest, exponent_bits=8, mantissa_bits=7)
+    low = rest - middle
+    return jnp.stack([high, middle, low]).astype(jnp.bfloat16)
+
+
+def squares_kernel(states_ref, squares_ref, copy_ref):
     spans, slots_n, _ = states_ref.shape
     for c in range(spans):
-        values = states_ref[c].astype(jnp.float32)
-        column = jnp.sum(values * values, axis=1, keepdims=True)
-        out_ref[pl.ds(c, 1), :] = jnp.transpose(jnp.broadcast_to(column, (slots_n, 128)))[:1, :]
+        values = states_ref[c]
+        copy_ref[c] = values
+        wide = values.astype(jnp.float32)
+        column = jnp.sum(wide * wide, axis=1, keepdims=True)
+        squares_ref[pl.ds(c, 1), :] = jnp.transpose(jnp.broadcast_to(column, (slots_n, 128)))[:1, :]
 
 
 def make_local(dp_shape):
@@ -69,8 +91,11 @@
 
     def local(states, valid_counts, section_ids, norm_gain, head_weight):
         local_spans, slots_n, features = states.shape
-        partial_squares = pl.pallas_call(
-            squares_kernel, out_shape=jax.ShapeDtypeStruct((local_spans, slots_n), jnp.float32)
+        vmem = pl.BlockSpec(memory_space=pltpu.VMEM)
+        partial_squares, resident = pl.pallas_call(
+            squares_kernel,
+            out_shape=(pltpu.VMEM((local_spans, slots_n), jnp.float32), pltpu.VMEM(states.shape, states.dtype)),
+            out_specs=(vmem, vmem),
         )(states)
         squares = fsdp_sum(partial_squares)
         sec_local = local_spans // 2
@@ -79,14 +104,21 @@
         vmem = pl.BlockSpec(memory_space=pltpu.VMEM)
         contrib = pl.pallas_call(
             functools.partial(pool_kernel, dp_shape),
-            out_shape=jax.ShapeDtypeStruct((total_sections, 1, features), jnp.float32),
+            out_shape=pltpu.VMEM((total_sections, 1, features), jnp.float32),
             in_specs=[smem, smem, vmem, vmem],
             out_specs=vmem,
-        )(valid_counts, section_ids, states, squares)
+        )(
+            valid_counts,
+            section_ids,
+            pltpu.with_memory_space_constraint(resident, pltpu.VMEM),
+            pltpu.with_memory_space_constraint(squares, pltpu.VMEM),
+        )
         received = lax.all_to_all(contrib, ("c", "xh", "z"), 0, 0, tiled=True)
         section_sums = jnp.sum(received.reshape(groups, sec_local, features), axis=0)
         section_sums = section_sums * norm_gain.astype(jnp.float32)[None, :]
-        terms = jnp.dot(section_sums, head_weight.astype(jnp.float32), precision=lax.Precision.HIGHEST)
+        parts = split3_rounded(section_sums)
+        stacked = jnp.dot(parts.reshape(-1, features), head_weight, preferred_element_type=jnp.float32)
+        terms = jnp.sum(stacked.reshape(3, sec_local, -1), axis=0)
         projected = fsdp_sum(terms)
         return nested(projected)
 

time: 75.4 us -> 72.1 us (0.956)
  Pallas kernels: 6.39 us -> 3.43 us
  blocking collectives: 67.4 us -> 66 us
  matrix products: 1.12 us -> 2.2 us
    pallas_call x3, Pallas kernels: 6.39 us -> 3.43 us  [the longest x1 1.77 us: local(): pl.pallas_call(squares_kernel, out_shape=(pltpu.VMEM((local_spans, slots_...]
    psum x4, blocking collectives: 35.1 us -> 33.8 us  [fsdp_sum(): return lax.psum(lax.psum(x, 'y'), 'xl')]
    dot_general x1, matrix products: 1.12 us -> 2.2 us  [local(): jnp.dot(parts.reshape(-1, features), head_weight, preferred_element_type=...]
where the time goes in v10:
time: 72.1 us; the launch traced here: 71.8 us
  blocking collectives  66 us (92%)
  Pallas kernels  3.43 us (5%)
  matrix products  2.2 us (3%)
    psum x4, blocking collectives, fsdp_sum(): return lax.psum(lax.psum(x, 'y'), 'xl')  33.8 us
    all_to_all x1, blocking collectives, local(): received = lax.all_to_all(contrib, ('c', 'xh', 'z'), 0, 0, tiled=True)  32.2 us
    dot_general x1, matrix products, local(): jnp.dot(parts.reshape(-1, features), head_weight, preferred_element_type=...  2.2 us
    pallas_call x1, Pallas kernels, local(): pl.pallas_call(squares_kernel, out_shape=(pltpu.VMEM((local_spans, slots_...  1.77 us

profile of v10, /device:TPU:8, one launch (start us, length us, event | category | flops | bytes accessed | tf_op | source)
XLA Modules:
  0.0 71.8 jit_solution(5734354721920358405)
XLA Ops:
  0.0 0.0 copy-start
  0.0 1.8 %shard_map.55 = (f32[2,512]{1,0:T(2,128)S(1)}, bf16[2,512,640]{2,1,0:T(8,128)(2,1)S(1)}) custom-call(bf16[2,512,640]{2,1,0:T(8,128)(2,1)} %states_ref.1), custom_call_target="tpu_custom_call" | custom-call | tf_op jit(solution)/shard_map/pallas_call | solution.py:95
  1.8 13.5 %psum.28 = f32[2,512]{1,0:T(2,128)S(1)} all-reduce(f32[2,512]{1,0:T(2,128)S(1)} %get-tuple-element.8), channel_id=1, replica_groups=mesh['z'=16,'xh'=2,'c'=2,'xl'=2,'y'=4] {'y'}, use_global_device_ids=true, to_apply=%region_0.0 | all-reduce | flops 1024 | bytes 8192 | tf_op jit(solution)/shard_map/psum | solution.py:37
  15.3 4.9 %psum.29.squares_ref = f32[2,512]{1,0:T(2,128)S(1)} all-reduce(f32[2,512]{1,0:T(2,128)S(1)} %psum.28), channel_id=1, replica_groups=mesh['z'=16,'xh'=2,'c'=2,'xl'=2,'y'=4] {'xl'}, use_global_device_ids=true, to_apply=%region_1.0 | all-reduce | flops 1024 | bytes 8192 | tf_op jit(solution)/shard_map/psum | solution.py:37
  20.2 1.0 %shard_map.56 = f32[64,1,640]{2,1,0:T(1,128)S(1)} custom-call(s32[2]{0:T(128)} %counts_ref.1, s32[128]{0:T(128)} %ids_ref.1, bf16[2,512,640]{2,1,0:T(8,128)(2,1)S(1)} %get-tuple-element.7.states_ref, f32[2,512]{1,0:T(2,128)S(1)} %psum.29.squares_ref), custom_call_target="tpu_custom_call" | custom-call | tf_op jit(solution)/shard_map/pallas_call | solution.py:105
  21.2 32.2 %all_to_all.5 = f32[64,1,640]{2,1,0:T(1,128)S(1)} all-to-all(f32[64,1,640]{2,1,0:T(1,128)S(1)} %shard_map.56), channel_id=1, replica_groups=mesh['z'=16,'xh'=2,'c'=2,'xl'=2,'y'=4] {'c','xh','z'}, dimensions={0} | all-to-all | bytes 327680 | tf_op jit(solution)/shard_map/all_to_all | solution.py:116
  53.4 0.1 reduce_sum.20
  53.5 0.0 copy-done
  53.5 2.2 %convolution_reduce_fusion = f32[2048]{0:T(1024)S(1)} fusion(bf16[640,2048]{1,0:T(8,128)(2,1)} %param.9, bf16[1,640]{1,0:T(2,128)(2,1)S(1)} %stack.14, bf16[1,640]{1,0:T(2,128)(2,1)S(1)} %stack.13, bf16[1,640]{1,0:T(2,128)(2,1)S(1)} %stack.12), kind=kOutput, calls=%fused_computation | convolution fusion | flops 7879936 | bytes 2633472 | tf_op jit(solution)/shard_map/dot_general | solution.py:120
  55.7 10.3 %psum.30 = f32[1,2048]{1,0:T(1,128)S(1)} all-reduce(f32[1,2048]{1,0:T(1,128)S(1)} %bitcast.2), channel_id=1, replica_groups=mesh['z'=16,'xh'=2,'c'=2,'xl'=2,'y'=4] {'y'}, use_global_device_ids=true, to_apply=%region_4.0 | all-reduce | flops 2048 | bytes 16384 | tf_op jit(solution)/shard_map/psum | solution.py:37
  66.1 5.0 %psum.31.x_ref = f32[1,2048]{1,0:T(1,128)S(1)} all-reduce(f32[1,2048]{1,0:T(1,128)S(1)} %psum.30), channel_id=1, replica_groups=mesh['z'=16,'xh'=2,'c'=2,'xl'=2,'y'=4] {'xl'}, use_global_device_ids=true, to_apply=%region_5.0 | all-reduce | flops 2048 | bytes 16384 | tf_op jit(solution)/shard_map/psum | solution.py:37
  71.1 0.7 shard_map.57
  (4 shorter events, 0.0 us)
Async XLA Ops:
  0.0 53.5 %copy-start = (bf16[640]{0:T(1024)(128)(2,1)S(1)}, bf16[640]{0:T(1024)(128)(2,1)}, u32[]{:S(2)}) copy-start(bf16[640]{0:T(1024)(128)(2,1)} %param.8) | copy-start | bytes 3844

commit v11 on v9

--- a/solution.py
+++ b/solution.py
@@ -37,32 +37,47 @@
     return lax.psum(lax.psum(x, "y"), "xl")
 
 
-def pool_kernel(dp_shape, counts_ref, ids_ref, states_ref, squares_ref, out_ref):
-    _, slots_n, _ = states_ref.shape
+def pool_kernel(dp_shape, counts_ref, ids_ref, states_ref, squares_ref, out_ref, acc_ref):
+    _, piece, _ = states_ref.shape
     spans = squares_ref.shape[0]
     z_n, xh_n, c_n = dp_shape
     sec_local = out_ref.shape[0] // (z_n * xh_n * c_n)
     me = (lax.axis_index("z") * xh_n + lax.axis_index("xh")) * c_n + lax.axis_index("c")
     c = pl.program_id(0)
+    h = pl.program_id(1)
+    last = pl.num_programs(1) - 1
 
-    @pl.when(c == 0)
+    @pl.when((c == 0) & (h == 0))
     def _():
         out_ref[...] = jnp.zeros(out_ref.shape, jnp.float32)
 
-    rows = lax.broadcasted_iota(jnp.int32, (8, slots_n), 0)
+    rows = lax.broadcasted_iota(jnp.int32, (8, piece), 0)
     count = counts_ref[c]
-    scale = lax.rsqrt(squares_ref[pl.ds(c, 1), :] / D + epsilon)
-    slots = lax.broadcasted_iota(jnp.int32, scale.shape, 1)
+    start = pl.multiple_of(h * piece, piece)
+    scale = lax.rsqrt(squares_ref[pl.ds(c, 1), pl.ds(start, piece)] / D + epsilon)
+    slots = lax.broadcasted_iota(jnp.int32, scale.shape, 1) + start
     weights = jnp.where(slots < count, scale, 0.0)
-    parts = jnp.where(rows < 3, split3(weights, rows), jnp.zeros((8, slots_n), jnp.bfloat16))
+    parts = jnp.where(rows < 3, split3(weights, rows), jnp.zeros((8, piece), jnp.bfloat16))
     partial = jnp.dot(parts, states_ref[0], preferred_element_type=jnp.float32)
-    sums = partial[0:1, :] + partial[1:2, :] + partial[2:3, :]
-    pooled = sums / count.astype(jnp.float32)
-    section = ids_ref[me * spans + c]
-    owner = section // sec_local
-    place = ((owner % c_n) * xh_n + (owner // c_n) % xh_n) * z_n + owner // (c_n * xh_n)
-    row = place * sec_local + section % sec_local
-    out_ref[pl.ds(row, 1)] += pooled[None]
+
+    @pl.when(h == 0)
+    def _():
+        acc_ref[...] = partial
+
+    @pl.when(h > 0)
+    def _():
+        acc_ref[...] += partial
+
+    @pl.when(h == last)
+    def _():
+        total = acc_ref[...]
+        sums = total[0:1, :] + total[1:2, :] + total[2:3, :]
+        pooled = sums / count.astype(jnp.float32)
+        section = ids_ref[me * spans + c]
+        owner = section // sec_local
+        place = ((owner % c_n) * xh_n + (owner // c_n) % xh_n) * z_n + owner // (c_n * xh_n)
+        row = place * sec_local + section % sec_local
+        out_ref[pl.ds(row, 1)] += pooled[None]
 
 
 def split3(x, rows):
@@ -96,14 +111,15 @@
         contrib = pl.pallas_call(
             functools.partial(pool_kernel, dp_shape),
             out_shape=pltpu.VMEM((total_sections, 1, features), jnp.float32),
-            grid=(local_spans,),
+            grid=(local_spans, 2),
             in_specs=[
                 smem,
                 smem,
-                pl.BlockSpec((1, slots_n, features), lambda c: (c, 0, 0)),
-                pl.BlockSpec((local_spans, slots_n), lambda c: (0, 0), memory_space=pltpu.VMEM),
+                pl.BlockSpec((1, slots_n // 2, features), lambda c, h: (c, h, 0)),
+                pl.BlockSpec((local_spans, slots_n), lambda c, h: (0, 0), memory_space=pltpu.VMEM),
             ],
-            out_specs=pl.BlockSpec((total_sections, 1, features), lambda c: (0, 0, 0), memory_space=pltpu.VMEM),
+            out_specs=pl.BlockSpec((total_sections, 1, features), lambda c, h: (0, 0, 0), memory_space=pltpu.VMEM),
+            scratch_shapes=[pltpu.VMEM((8, features), jnp.float32)],
         )(valid_counts, section_ids, states, pltpu.with_memory_space_constraint(squares, pltpu.VMEM))
         received = lax.all_to_all(contrib, ("c", "xh", "z"), 0, 0, tiled=True)
         section_sums = jnp.sum(received.reshape(groups, sec_local, features), axis=0)

time: 71 us -> 72.1 us (1.015)
  Pallas kernels: 2.27 us -> 3.36 us
    pallas_call x1, Pallas kernels: 1.56 us -> 2.65 us  [local(): pl.pallas_call(functools.partial(pool_kernel, dp_shape), out_shape=pltpu....]
where the time goes in v11:
time: 72.1 us; the launch traced here: 71.8 us
  blocking collectives  66 us (92%)
  Pallas kernels  3.36 us (5%)
  other arithmetic  1.95 us (3%)
    psum x4, blocking collectives, fsdp_sum(): return lax.psum(lax.psum(x, 'y'), 'xl')  33.8 us
    all_to_all x1, blocking collectives, local(): received = lax.all_to_all(contrib, ('c', 'xh', 'z'), 0, 0, tiled=True)  32.2 us
    pallas_call x1, Pallas kernels, local(): pl.pallas_call(functools.partial(pool_kernel, dp_shape), out_shape=pltpu....  2.65 us
    reduce_sum x1, other arithmetic, local(): partial_squares = jnp.sum(values * values, axis=-1)  1.81 us

profile of v11, /device:TPU:8, one launch (start us, length us, event | category | flops | bytes accessed | tf_op | source)
XLA Modules:
  0.0 71.8 jit_solution(9951250113115711828)
XLA Ops:
  0.0 0.0 copy-start
  0.0 0.0 copy-start.1
  0.0 1.8 %multiply_reduce_fusion = f32[2,512]{1,0:T(2,128)S(1)} fusion(bf16[2,512,640]{2,1,0:T(8,128)(2,1)} %states_ref.1), kind=kLoop, calls=%fused_computation | loop fusion | flops 1965056 | bytes 1314816 | tf_op jit(solution)/shard_map/reduce_sum | solution.py:104
  1.8 13.6 %psum.28 = f32[2,512]{1,0:T(2,128)S(1)} all-reduce(f32[2,512]{1,0:T(2,128)S(1)} %multiply_reduce_fusion), channel_id=1, replica_groups=mesh['z'=16,'xh'=2,'c'=2,'xl'=2,'y'=4] {'y'}, use_global_device_ids=true, to_apply=%region_1.0 | all-reduce | flops 1024 | bytes 8192 | tf_op jit(solution)/shard_map/psum | solution.py:37
  15.4 4.9 %psum.29.squares_ref = f32[2,512]{1,0:T(2,128)S(1)} all-reduce(f32[2,512]{1,0:T(2,128)S(1)} %psum.28), channel_id=1, replica_groups=mesh['z'=16,'xh'=2,'c'=2,'xl'=2,'y'=4] {'xl'}, use_global_device_ids=true, to_apply=%region_2.0 | all-reduce | flops 1024 | bytes 8192 | tf_op jit(solution)/shard_map/psum | solution.py:37
  20.3 2.7 %shard_map.55 = f32[64,1,640]{2,1,0:T(1,128)S(1)} custom-call(s32[2]{0:T(128)} %counts_ref.1, s32[128]{0:T(128)} %ids_ref.1, bf16[2,512,640]{2,1,0:T(8,128)(2,1)} %states_ref.1, f32[2,512]{1,0:T(2,128)S(1)} %psum.29.squares_ref), custom_call_target="tpu_custom_call" | custom-call | tf_op jit(solution)/shard_map/pallas_call | solution.py:111
  23.0 32.2 %all_to_all.5 = f32[64,1,640]{2,1,0:T(1,128)S(1)} all-to-all(f32[64,1,640]{2,1,0:T(1,128)S(1)} %shard_map.55), channel_id=1, replica_groups=mesh['z'=16,'xh'=2,'c'=2,'xl'=2,'y'=4] {'c','xh','z'}, dimensions={0} | all-to-all | bytes 327680 | tf_op jit(solution)/shard_map/all_to_all | solution.py:124
  55.1 0.1 reduce_sum.30
  55.2 0.0 copy-done.1
  55.3 0.0 copy-done
  55.3 0.5 convolution_reduce_fusion
  55.8 10.3 %psum.30 = f32[1,2048]{1,0:T(1,128)S(1)} all-reduce(f32[1,2048]{1,0:T(1,128)S(1)} %bitcast.2), channel_id=1, replica_groups=mesh['z'=16,'xh'=2,'c'=2,'xl'=2,'y'=4] {'y'}, use_global_device_ids=true, to_apply=%region_5.0 | all-reduce | flops 2048 | bytes 16384 | tf_op jit(solution)/shard_map/psum | solution.py:37
  66.1 5.0 %psum.31.x_ref = f32[1,2048]{1,0:T(1,128)S(1)} all-reduce(f32[1,2048]{1,0:T(1,128)S(1)} %psum.30), channel_id=1, replica_groups=mesh['z'=16,'xh'=2,'c'=2,'xl'=2,'y'=4] {'xl'}, use_global_device_ids=true, to_apply=%region_6.0 | all-reduce | flops 2048 | bytes 16384 | tf_op jit(solution)/shard_map/psum | solution.py:37
  71.1 0.7 shard_map.56
  (4 shorter events, 0.0 us)
Async XLA Ops:
  0.0 55.3 %copy-start = (bf16[640,2048]{1,0:T(8,128)(2,1)S(1)}, bf16[640,2048]{1,0:T(8,128)(2,1)}, u32[]{:S(2)}) copy-start(bf16[640,2048]{1,0:T(8,128)(2,1)} %param.9) | copy-start | bytes 7864324
  0.0 55.2 %copy-start.1 = (bf16[640]{0:T(1024)(128)(2,1)S(1)}, bf16[640]{0:T(1024)(128)(2,1)}, u32[]{:S(2)}) copy-start(bf16[640]{0:T(1024)(128)(2,1)} %param.8) | copy-start | bytes 3844

commit v12 on v10

--- a/solution.py
+++ b/solution.py
@@ -76,28 +76,14 @@
     return jnp.stack([high, middle, low]).astype(jnp.bfloat16)
 
 
-def squares_kernel(states_ref, squares_ref, copy_ref):
-    spans, slots_n, _ = states_ref.shape
-    for c in range(spans):
-        values = states_ref[c]
-        copy_ref[c] = values
-        wide = values.astype(jnp.float32)
-        column = jnp.sum(wide * wide, axis=1, keepdims=True)
-        squares_ref[pl.ds(c, 1), :] = jnp.transpose(jnp.broadcast_to(column, (slots_n, 128)))[:1, :]
-
-
 def make_local(dp_shape):
     groups = dp_shape[0] * dp_shape[1] * dp_shape[2]
 
     def local(states, valid_counts, section_ids, norm_gain, head_weight):
+        values = states.astype(jnp.float32)
+        partial_squares = jnp.sum(values * values, axis=-1)
+        squares = fsdp_sum(partial_squares)
         local_spans, slots_n, features = states.shape
-        vmem = pl.BlockSpec(memory_space=pltpu.VMEM)
-        partial_squares, resident = pl.pallas_call(
-            squares_kernel,
-            out_shape=(pltpu.VMEM((local_spans, slots_n), jnp.float32), pltpu.VMEM(states.shape, states.dtype)),
-            out_specs=(vmem, vmem),
-        )(states)
-        squares = fsdp_sum(partial_squares)
         sec_local = local_spans // 2
         total_sections = sec_local * groups
         smem = pl.BlockSpec(memory_space=pltpu.SMEM)
@@ -107,12 +93,7 @@
             out_shape=pltpu.VMEM((total_sections, 1, features), jnp.float32),
             in_specs=[smem, smem, vmem, vmem],
             out_specs=vmem,
-        )(
-            valid_counts,
-            section_ids,
-            pltpu.with_memory_space_constraint(resident, pltpu.VMEM),
-            pltpu.with_memory_space_constraint(squares, pltpu.VMEM),
-        )
+        )(valid_counts, section_ids, states, pltpu.with_memory_space_constraint(squares, pltpu.VMEM))
         received = lax.all_to_all(contrib, ("c", "xh", "z"), 0, 0, tiled=True)
         section_sums = jnp.sum(received.reshape(groups, sec_local, features), axis=0)
         section_sums = section_sums * norm_gain.astype(jnp.float32)[None, :]

time: 72.1 us -> 71 us (0.985)
  other arithmetic: 0.14 us -> 1.95 us
  matrix products: 2.2 us -> 0.46 us
  Pallas kernels: 3.43 us -> 2.31 us
    reduce_sum x0 -> x1, other arithmetic: none -> 1.81 us  [local(): partial_squares = jnp.sum(values * values, axis=-1)]
    pallas_call x1 -> x0, Pallas kernels: 1.77 us -> none  [local(): pl.pallas_call(squares_kernel, out_shape=(pltpu.VMEM((local_spans, slots_...]
    dot_general x1, matrix products: 2.2 us -> 0.46 us  [local(): jnp.dot(parts.reshape(-1, features), head_weight, preferred_element_type=...]
where the time goes in v12:
time: 71 us; the launch traced here: 70.8 us
  blocking collectives  66 us (93%)
  Pallas kernels  2.31 us (3%)
  other arithmetic  1.95 us (3%)
    psum x4, blocking collectives, fsdp_sum(): return lax.psum(lax.psum(x, 'y'), 'xl')  33.8 us
    all_to_all x1, blocking collectives, local(): received = lax.all_to_all(contrib, ('c', 'xh', 'z'), 0, 0, tiled=True)  32.2 us
    reduce_sum x1, other arithmetic, local(): partial_squares = jnp.sum(values * values, axis=-1)  1.81 us
    pallas_call x1, Pallas kernels, local(): pl.pallas_call(functools.partial(pool_kernel, dp_shape), out_shape=pltpu....  1.61 us

profile of v12, /device:TPU:8, one launch (start us, length us, event | category | flops | bytes accessed | tf_op | source)
XLA Modules:
  0.0 70.8 jit_solution(5698631713514374963)
XLA Ops:
  0.0 0.0 copy-start
  0.0 0.0 copy-start.1
  0.0 1.8 %multiply_reduce_fusion = f32[2,512]{1,0:T(2,128)S(1)} fusion(bf16[2,512,640]{2,1,0:T(8,128)(2,1)} %states_ref.1), kind=kLoop, calls=%fused_computation | loop fusion | flops 1965056 | bytes 1314816 | tf_op jit(solution)/shard_map/reduce_sum | solution.py:84
  1.8 13.6 %psum.28 = f32[2,512]{1,0:T(2,128)S(1)} all-reduce(f32[2,512]{1,0:T(2,128)S(1)} %multiply_reduce_fusion), channel_id=1, replica_groups=mesh['z'=16,'xh'=2,'c'=2,'xl'=2,'y'=4] {'y'}, use_global_device_ids=true, to_apply=%region_1.0 | all-reduce | flops 1024 | bytes 8192 | tf_op jit(solution)/shard_map/psum | solution.py:37
  15.4 4.9 %psum.29.squares_ref = f32[2,512]{1,0:T(2,128)S(1)} all-reduce(f32[2,512]{1,0:T(2,128)S(1)} %psum.28), channel_id=1, replica_groups=mesh['z'=16,'xh'=2,'c'=2,'xl'=2,'y'=4] {'xl'}, use_global_device_ids=true, to_apply=%region_2.0 | all-reduce | flops 1024 | bytes 8192 | tf_op jit(solution)/shard_map/psum | solution.py:37
  20.3 1.6 %shard_map.55 = f32[64,1,640]{2,1,0:T(1,128)S(1)} custom-call(s32[2]{0:T(128)} %counts_ref.1, s32[128]{0:T(128)} %ids_ref.1, bf16[2,512,640]{2,1,0:T(8,128)(2,1)} %states_ref.1, f32[2,512]{1,0:T(2,128)S(1)} %psum.29.squares_ref), custom_call_target="tpu_custom_call" | custom-call | tf_op jit(solution)/shard_map/pallas_call | solution.py:91
  21.9 32.2 %all_to_all.5 = f32[64,1,640]{2,1,0:T(1,128)S(1)} all-to-all(f32[64,1,640]{2,1,0:T(1,128)S(1)} %shard_map.55), channel_id=1, replica_groups=mesh['z'=16,'xh'=2,'c'=2,'xl'=2,'y'=4] {'c','xh','z'}, dimensions={0} | all-to-all | bytes 327680 | tf_op jit(solution)/shard_map/all_to_all | solution.py:97
  54.1 0.1 reduce_sum.30
  54.2 0.0 copy-done.1
  54.3 0.0 copy-done
  54.3 0.5 convolution_reduce_fusion
  54.7 10.3 %psum.30 = f32[1,2048]{1,0:T(1,128)S(1)} all-reduce(f32[1,2048]{1,0:T(1,128)S(1)} %bitcast.2), channel_id=1, replica_groups=mesh['z'=16,'xh'=2,'c'=2,'xl'=2,'y'=4] {'y'}, use_global_device_ids=true, to_apply=%region_5.0 | all-reduce | flops 2048 | bytes 16384 | tf_op jit(solution)/shard_map/psum | solution.py:37
  65.1 5.0 %psum.31.x_ref = f32[1,2048]{1,0:T(1,128)S(1)} all-reduce(f32[1,2048]{1,0:T(1,128)S(1)} %psum.30), channel_id=1, replica_groups=mesh['z'=16,'xh'=2,'c'=2,'xl'=2,'y'=4] {'xl'}, use_global_device_ids=true, to_apply=%region_6.0 | all-reduce | flops 2048 | bytes 16384 | tf_op jit(solution)/shard_map/psum | solution.py:37
  70.1 0.7 shard_map.56
  (4 shorter events, 0.0 us)
Async XLA Ops:
  0.0 54.3 %copy-start = (bf16[640,2048]{1,0:T(8,128)(2,1)S(1)}, bf16[640,2048]{1,0:T(8,128)(2,1)}, u32[]{:S(2)}) copy-start(bf16[640,2048]{1,0:T(8,128)(2,1)} %param.9) | copy-start | bytes 7864324
  0.0 54.2 %copy-start.1 = (bf16[640]{0:T(1024)(128)(2,1)S(1)}, bf16[640]{0:T(1024)(128)(2,1)}, u32[]{:S(2)}) copy-start(bf16[640]{0:T(1024)(128)(2,1)} %param.8) | copy-start | bytes 3844

commit v13 on v9

--- a/solution.py
+++ b/solution.py
@@ -111,7 +111,7 @@
         parts = split3_rounded(section_sums)
         stacked = jnp.dot(parts.reshape(-1, features), head_weight, preferred_element_type=jnp.float32)
         terms = jnp.sum(stacked.reshape(3, sec_local, -1), axis=0)
-        projected = fsdp_sum(terms)
+        projected = fsdp_sum(terms.reshape(-1, 128)).reshape(terms.shape)
         return nested(projected)
 
     return local

time: 71 us -> 71 us (level)
  no operation moved by 1% of the time
where the time goes in v13:
time: 71 us; the launch traced here: 70.7 us
  blocking collectives  66 us (93%)
  Pallas kernels  2.27 us (3%)
  other arithmetic  1.95 us (3%)
    psum x4, blocking collectives, fsdp_sum(): return lax.psum(lax.psum(x, 'y'), 'xl')  33.8 us
    all_to_all x1, blocking collectives, local(): received = lax.all_to_all(contrib, ('c', 'xh', 'z'), 0, 0, tiled=True)  32.2 us
    reduce_sum x1, other arithmetic, local(): partial_squares = jnp.sum(values * values, axis=-1)  1.81 us
    pallas_call x1, Pallas kernels, local(): pl.pallas_call(functools.partial(pool_kernel, dp_shape), out_shape=pltpu....  1.56 us

profile of v13, /device:TPU:8, one launch (start us, length us, event | category | flops | bytes accessed | tf_op | source)
XLA Modules:
  0.0 70.7 jit_solution(13016947049312298295)
XLA Ops:
  0.0 0.0 copy-start
  0.0 0.0 copy-start.1
  0.0 1.8 %multiply_reduce_fusion = f32[2,512]{1,0:T(2,128)S(1)} fusion(bf16[2,512,640]{2,1,0:T(8,128)(2,1)} %states_ref.1), kind=kLoop, calls=%fused_computation | loop fusion | flops 1965056 | bytes 1314816 | tf_op jit(solution)/shard_map/reduce_sum | solution.py:89
  1.8 13.6 %psum.28 = f32[2,512]{1,0:T(2,128)S(1)} all-reduce(f32[2,512]{1,0:T(2,128)S(1)} %multiply_reduce_fusion), channel_id=1, replica_groups=mesh['z'=16,'xh'=2,'c'=2,'xl'=2,'y'=4] {'y'}, use_global_device_ids=true, to_apply=%region_1.0 | all-reduce | flops 1024 | bytes 8192 | tf_op jit(solution)/shard_map/psum | solution.py:37
  15.4 4.9 %psum.29.squares_ref = f32[2,512]{1,0:T(2,128)S(1)} all-reduce(f32[2,512]{1,0:T(2,128)S(1)} %psum.28), channel_id=1, replica_groups=mesh['z'=16,'xh'=2,'c'=2,'xl'=2,'y'=4] {'xl'}, use_global_device_ids=true, to_apply=%region_2.0 | all-reduce | flops 1024 | bytes 8192 | tf_op jit(solution)/shard_map/psum | solution.py:37
  20.3 1.6 %shard_map.55 = f32[64,1,640]{2,1,0:T(1,128)S(1)} custom-call(s32[2]{0:T(128)} %counts_ref.1, s32[128]{0:T(128)} %ids_ref.1, bf16[2,512,640]{2,1,0:T(8,128)(2,1)} %states_ref.1, f32[2,512]{1,0:T(2,128)S(1)} %psum.29.squares_ref), custom_call_target="tpu_custom_call" | custom-call | tf_op jit(solution)/shard_map/pallas_call | solution.py:96
  21.9 32.2 %all_to_all.5 = f32[64,1,640]{2,1,0:T(1,128)S(1)} all-to-all(f32[64,1,640]{2,1,0:T(1,128)S(1)} %shard_map.55), channel_id=1, replica_groups=mesh['z'=16,'xh'=2,'c'=2,'xl'=2,'y'=4] {'c','xh','z'}, dimensions={0} | all-to-all | bytes 327680 | tf_op jit(solution)/shard_map/all_to_all | solution.py:108
  54.0 0.1 reduce_sum.28
  54.2 0.0 copy-done.1
  54.2 0.0 copy-done
  54.2 0.5 convolution_reduce_fusion
  54.7 10.3 %psum.30 = f32[16,128]{1,0:T(8,128)S(1)} all-reduce(f32[16,128]{1,0:T(8,128)S(1)} %bitcast.3), channel_id=1, replica_groups=mesh['z'=16,'xh'=2,'c'=2,'xl'=2,'y'=4] {'y'}, use_global_device_ids=true, to_apply=%region_5.0 | all-reduce | flops 2048 | bytes 16384 | tf_op jit(solution)/shard_map/psum | solution.py:37
  65.0 5.0 %psum.31.x_ref = f32[1,2048]{1,0:T(1,128)S(1)} all-reduce(f32[1,2048]{1,0:T(1,128)S(1)} %bitcast.4), channel_id=1, replica_groups=mesh['z'=16,'xh'=2,'c'=2,'xl'=2,'y'=4] {'xl'}, use_global_device_ids=true, to_apply=%region_6.0 | all-reduce | flops 2048 | bytes 16384 | tf_op jit(solution)/shard_map/psum | solution.py:37
  70.0 0.7 shard_map.56
  (4 shorter events, 0.0 us)
Async XLA Ops:
  0.0 54.2 %copy-start = (bf16[640,2048]{1,0:T(8,128)(2,1)S(1)}, bf16[640,2048]{1,0:T(8,128)(2,1)}, u32[]{:S(2)}) copy-start(bf16[640,2048]{1,0:T(8,128)(2,1)} %param.9) | copy-start | bytes 7864324
  0.0 54.2 %copy-start.1 = (bf16[640]{0:T(1024)(128)(2,1)S(1)}, bf16[640]{0:T(1024)(128)(2,1)}, u32[]{:S(2)}) copy-start(bf16[640]{0:T(1024)(128)(2,1)} %param.8) | copy-start | bytes 3844

commit v14 on v9

--- a/solution.py
+++ b/solution.py
@@ -81,12 +81,24 @@
     return jnp.stack([high, middle, low]).astype(jnp.bfloat16)
 
 
+def squares_kernel(states_ref, squares_ref):
+    spans, slots_n, _ = states_ref.shape
+    for c in range(spans):
+        wide = states_ref[c].astype(jnp.float32)
+        column = jnp.sum(wide * wide, axis=1, keepdims=True)
+        squares_ref[pl.ds(c, 1), :] = jnp.transpose(jnp.broadcast_to(column, (slots_n, 128)))[:1, :]
+
+
 def make_local(dp_shape):
     groups = dp_shape[0] * dp_shape[1] * dp_shape[2]
 
     def local(states, valid_counts, section_ids, norm_gain, head_weight):
-        values = states.astype(jnp.float32)
-        partial_squares = jnp.sum(values * values, axis=-1)
+        local_spans, slots_n, features = states.shape
+        partial_squares = pl.pallas_call(
+            squares_kernel,
+            out_shape=pltpu.VMEM((local_spans, slots_n), jnp.float32),
+            out_specs=pl.BlockSpec(memory_space=pltpu.VMEM),
+        )(states)
         squares = fsdp_sum(partial_squares)
         local_spans, slots_n, features = states.shape
         sec_local = local_spans // 2

time: 71 us -> 71 us (level)
  Pallas kernels: 2.27 us -> 4.18 us
  other arithmetic: 1.95 us -> 0.14 us
    pallas_call x0 -> x1, Pallas kernels: none -> 1.9 us  [local(): pl.pallas_call(squares_kernel, out_shape=pltpu.VMEM((local_spans, slots_n...]
    reduce_sum x1 -> x0, other arithmetic: 1.81 us -> none  [local(): partial_squares = jnp.sum(values * values, axis=-1)]
where the time goes in v14:
time: 71 us; the launch traced here: 70.8 us
  blocking collectives  66 us (93%)
  Pallas kernels  4.18 us (6%)
    psum x4, blocking collectives, fsdp_sum(): return lax.psum(lax.psum(x, 'y'), 'xl')  33.8 us
    all_to_all x1, blocking collectives, local(): received = lax.all_to_all(contrib, ('c', 'xh', 'z'), 0, 0, tiled=True)  32.2 us
    pallas_call x1, Pallas kernels, local(): pl.pallas_call(squares_kernel, out_shape=pltpu.VMEM((local_spans, slots_n...  1.9 us
    pallas_call x1, Pallas kernels, local(): pl.pallas_call(functools.partial(pool_kernel, dp_shape), out_shape=pltpu....  1.56 us

profile of v14, /device:TPU:8, one launch (start us, length us, event | category | flops | bytes accessed | tf_op | source)
XLA Modules:
  0.0 70.8 jit_solution(5695119194945542996)
XLA Ops:
  0.0 0.0 copy-start
  0.0 0.0 copy-start.1
  0.0 1.9 %shard_map.55 = f32[2,512]{1,0:T(2,128)S(1)} custom-call(bf16[2,512,640]{2,1,0:T(8,128)(2,1)} %states_ref.3), custom_call_target="tpu_custom_call" | custom-call | tf_op jit(solution)/shard_map/pallas_call | solution.py:97
  1.9 13.5 %psum.28 = f32[2,512]{1,0:T(2,128)S(1)} all-reduce(f32[2,512]{1,0:T(2,128)S(1)} %shard_map.55), channel_id=1, replica_groups=mesh['z'=16,'xh'=2,'c'=2,'xl'=2,'y'=4] {'y'}, use_global_device_ids=true, to_apply=%region_0.0 | all-reduce | flops 1024 | bytes 8192 | tf_op jit(solution)/shard_map/psum | solution.py:37
  15.4 4.9 %psum.29.squares_ref = f32[2,512]{1,0:T(2,128)S(1)} all-reduce(f32[2,512]{1,0:T(2,128)S(1)} %psum.28), channel_id=1, replica_groups=mesh['z'=16,'xh'=2,'c'=2,'xl'=2,'y'=4] {'xl'}, use_global_device_ids=true, to_apply=%region_1.0 | all-reduce | flops 1024 | bytes 8192 | tf_op jit(solution)/shard_map/psum | solution.py:37
  20.4 1.6 %shard_map.56 = f32[64,1,640]{2,1,0:T(1,128)S(1)} custom-call(s32[2]{0:T(128)} %counts_ref.1, s32[128]{0:T(128)} %ids_ref.1, bf16[2,512,640]{2,1,0:T(8,128)(2,1)} %states_ref.3, f32[2,512]{1,0:T(2,128)S(1)} %psum.29.squares_ref), custom_call_target="tpu_custom_call" | custom-call | tf_op jit(solution)/shard_map/pallas_call | solution.py:108
  22.0 32.2 %all_to_all.5 = f32[64,1,640]{2,1,0:T(1,128)S(1)} all-to-all(f32[64,1,640]{2,1,0:T(1,128)S(1)} %shard_map.56), channel_id=1, replica_groups=mesh['z'=16,'xh'=2,'c'=2,'xl'=2,'y'=4] {'c','xh','z'}, dimensions={0} | all-to-all | bytes 327680 | tf_op jit(solution)/shard_map/all_to_all | solution.py:120
  54.1 0.1 reduce_sum.20
  54.2 0.0 copy-done.1
  54.3 0.0 copy-done
  54.3 0.5 convolution_reduce_fusion
  54.8 10.3 %psum.30 = f32[1,2048]{1,0:T(1,128)S(1)} all-reduce(f32[1,2048]{1,0:T(1,128)S(1)} %bitcast.2), channel_id=1, replica_groups=mesh['z'=16,'xh'=2,'c'=2,'xl'=2,'y'=4] {'y'}, use_global_device_ids=true, to_apply=%region_4.0 | all-reduce | flops 2048 | bytes 16384 | tf_op jit(solution)/shard_map/psum | solution.py:37
  65.1 5.0 %psum.31.x_ref = f32[1,2048]{1,0:T(1,128)S(1)} all-reduce(f32[1,2048]{1,0:T(1,128)S(1)} %psum.30), channel_id=1, replica_groups=mesh['z'=16,'xh'=2,'c'=2,'xl'=2,'y'=4] {'xl'}, use_global_device_ids=true, to_apply=%region_5.0 | all-reduce | flops 2048 | bytes 16384 | tf_op jit(solution)/shard_map/psum | solution.py:37
  70.1 0.7 shard_map.57
  (4 shorter events, 0.0 us)
Async XLA Ops:
  0.0 54.3 %copy-start = (bf16[640,2048]{1,0:T(8,128)(2,1)S(1)}, bf16[640,2048]{1,0:T(8,128)(2,1)}, u32[]{:S(2)}) copy-start(bf16[640,2048]{1,0:T(8,128)(2,1)} %param.9) | copy-start | bytes 7864324
  0.0 54.2 %copy-start.1 = (bf16[640]{0:T(1024)(128)(2,1)S(1)}, bf16[640]{0:T(1024)(128)(2,1)}, u32[]{:S(2)}) copy-start(bf16[640]{0:T(1024)(128)(2,1)} %param.8) | copy-start | bytes 3844
